TPU v7x, 32 devices: a whole 2x2x4 slice. The times are simulated.
32 devices in a mesh: shard: 4 (over z), ctx: 4 (over y, x), tp: 2 (over core).
Axes of the slice: x: 2, y: 2, z: 4, core: 2. Of those that a mesh axis runs over, the one named last changes fastest.
Arguments:
- hidden_in: bfloat16 [24, 680, 1024], P('shard', 'ctx'), may hold values from -6 to 6
- cond: bfloat16 [24, 1024], P('shard'), may hold values from -6 to 6
- scale_len: int32 [24, 10], P('shard'), may hold values from 1 to 256, 680 in all within a row
- ada_weight: bfloat16 [1024, 6, 1024], P('shard'), may hold values from -0.1875 to 0.1875
- ada_bias: float32 [6, 1024], replicated, may hold values from -3 to 3
- qkv_weight: bfloat16 [1024, 3, 1024], P('shard', None, 'tp'), may hold values from -0.1875 to 0.1875
- query_bias: float32 [1024], P('tp'), may hold values from -3 to 3
- value_bias: float32 [1024], P('tp'), may hold values from -3 to 3
- head_scale: float32 [16], P('tp'), may hold values from 2 to 3
- proj_weight: bfloat16 [1024, 1024], P('tp', 'shard'), may hold values from -0.5 to 0.5
- proj_bias: float32 [1024], replicated, may hold values from -2 to 2
- up_weight: bfloat16 [1024, 4096], P('shard', 'tp'), may hold values from -0.1875 to 0.1875
- up_bias: float32 [4096], P('tp'), may hold values from -3 to 3
- down_weight: bfloat16 [4096, 1024], P('tp', 'shard'), may hold values from -0.125 to 0.125
- down_bias: float32 [1024], replicated, may hold values from -2 to 2
- out_grad: bfloat16 [24, 680, 1024], P('shard', 'ctx'), may hold values from -6 to 6
Outputs:
- hidden_out: bfloat16 [24, 680, 1024], P('shard', 'ctx')
- grad_hidden: bfloat16 [24, 680, 1024], P('shard', 'ctx')
- grad_cond: float32 [24, 1024], P('shard')
- grad_ada_weight: float32 [1024, 6, 1024], P('shard')
- grad_ada_bias: float32 [6, 1024], replicated
- grad_qkv_weight: float32 [1024, 3, 1024], P('shard', None, 'tp')
- grad_query_bias: float32 [1024], P('tp')
- grad_value_bias: float32 [1024], P('tp')
- grad_head_scale: float32 [16], P('tp')
- grad_proj_weight: float32 [1024, 1024], P('tp', 'shard')
- grad_proj_bias: float32 [1024], replicated
- grad_up_weight: float32 [1024, 4096], P('shard', 'tp')
- grad_up_bias: float32 [4096], P('tp')
- grad_down_weight: float32 [4096, 1024], P('tp', 'shard')
- grad_down_bias: float32 [1024], replicated
- norm_stats: float32 [3], replicated
Inputs may be any that keep to these rules, and one draw needn't show every extreme that they name: `scale_len`: each row holds the token counts of one map's 10 scales in order; they sum to 680, and the largest in every row is 256.
All inputs are finite; a program needn't handle non-finite values.
Results may differ from a plain program's by a relative error of at most 0.03.
Values may be sent and summed in bfloat16 or wider, within the bound.
No kernel may reach another device: no remote copies, remote signals or barrier semaphores. Data moves between devices by JAX's collectives and lax.ppermute only.
A program may use at most 256 MiB of HBM per device.

v0:
```python
import jax
import jax.numpy as jnp
from jax import lax
from jax.sharding import PartitionSpec as P


def layer_norm(values):
    center = values - jnp.mean(values, axis=-1, keepdims=True)
    spread = jnp.mean(center * center, axis=-1, keepdims=True)
    return center * lax.rsqrt(spread + 1e-06)


def modulate(values, scale, shift):
    return layer_norm(values) * (1.0 + scale[:, None, :]) + shift[:, None, :]


def unit_scaled(values, gains):
    normed = values * lax.rsqrt(jnp.sum(values * values, axis=-1, keepdims=True) + 1e-06)
    return normed * jnp.exp(gains)[None, None, :, None]


def unit_plain(values):
    return values * lax.rsqrt(jnp.sum(values * values, axis=-1, keepdims=True) + 1e-06)


def gelu_tanh(values):
    return jax.nn.gelu(values, approximate=True)


def tp_sum(values):
    count = lax.axis_size("tp")
    if count != 2:
        return lax.psum(values, "tp")
    return values + lax.ppermute(values, "tp", [(0, 1), (1, 0)])


def ctx_shifts(values):
    count = lax.axis_size("ctx")
    parts = [values]
    for shift in range(1, count):
        pairs = [(i, (i + shift) % count) for i in range(count)]
        parts.append(lax.ppermute(values, "ctx", pairs))
    return jnp.stack(parts)


def ctx_return(parts):
    count = lax.axis_size("ctx")
    total = parts[0].astype(jnp.float32)
    for shift in range(1, count):
        pairs = [(i, (i - shift) % count) for i in range(count)]
        total = total + lax.ppermute(parts[shift], "ctx", pairs).astype(jnp.float32)
    return total


def body(
    hidden_in,
    cond,
    scale_len,
    ada_weight,
    ada_bias,
    qkv_weight,
    query_bias,
    value_bias,
    head_scale,
    proj_weight,
    proj_bias,
    up_weight,
    up_bias,
    down_weight,
    down_bias,
    out_grad,
):
    map_count = hidden_in.shape[0]
    piece_rows = hidden_in.shape[1]
    model_width = hidden_in.shape[2]
    ctx_count = lax.axis_size("ctx")
    ctx_index = lax.axis_index("ctx")
    shard_index = lax.axis_index("shard")
    map_length = piece_rows * ctx_count
    heads_here = head_scale.shape[0]
    local_width = query_bias.shape[0]
    head_dim = local_width // heads_here
    row_count = map_count * piece_rows
    head_shape = (map_count, piece_rows, heads_here, head_dim)
    ada_rows = ada_weight.shape[0]
    full_qkv, full_up, full_proj, full_down = (
        lax.all_gather(qkv_weight, "shard", axis=0, tiled=True),
        lax.all_gather(up_weight, "shard", axis=0, tiled=True),
        lax.all_gather(proj_weight, "shard", axis=1, tiled=True),
        lax.all_gather(down_weight, "shard", axis=1, tiled=True),
    )
    qkv_matrix = full_qkv.reshape(model_width, 3 * local_width)
    cond_wide = cond.astype(jnp.float32)
    cond_all = lax.all_gather(cond, "shard", axis=0, tiled=True).astype(jnp.float32)
    cond_in_all = jax.nn.silu(cond_all).astype(jnp.bfloat16)
    cond_cols = lax.dynamic_slice_in_dim(cond_in_all, shard_index * ada_rows, ada_rows, axis=1)
    ada_local = ada_weight.reshape(ada_rows, 6 * model_width)
    mod_partial = jnp.dot(cond_cols, ada_local, preferred_element_type=jnp.float32)
    modulation = lax.psum_scatter(mod_partial, "shard", scatter_dimension=0, tiled=True)
    modulation = modulation.reshape(map_count, 6, model_width) + ada_bias[None]
    gamma_one = modulation[:, 0]
    gamma_two = modulation[:, 1]
    scale_one = modulation[:, 2]
    scale_two = modulation[:, 3]
    shift_one = modulation[:, 4]
    shift_two = modulation[:, 5]
    stream_in = hidden_in.astype(jnp.float32)
    first_mod, first_back = jax.vjp(modulate, stream_in, scale_one, shift_one)
    attn_in = first_mod.astype(jnp.bfloat16).reshape(row_count, model_width)
    qkv = jnp.dot(attn_in, qkv_matrix, preferred_element_type=jnp.float32).reshape(
        map_count, piece_rows, 3, local_width
    )
    query = (qkv[:, :, 0] + query_bias).reshape(head_shape)
    key_raw = qkv[:, :, 1].reshape(head_shape)
    value_low = (qkv[:, :, 2] + value_bias).astype(jnp.bfloat16).reshape(head_shape)
    query_unit, query_back = jax.vjp(unit_scaled, query, head_scale)
    key_unit, key_back = jax.vjp(unit_plain, key_raw)
    query_low = query_unit.astype(jnp.bfloat16)
    key_low = key_unit.astype(jnp.bfloat16)
    keys_parts = ctx_shifts(key_low)
    values_parts = ctx_shifts(value_low)
    scale_ends = jnp.cumsum(scale_len, axis=1)
    query_pos = ctx_index * piece_rows + jnp.arange(piece_rows, dtype=jnp.int32)
    visible_end = jnp.min(
        jnp.where(
            scale_ends[:, None, :] > query_pos[None, :, None], scale_ends[:, None, :], map_length
        ),
        axis=2,
    )
    owners = (ctx_index - jnp.arange(ctx_count, dtype=jnp.int32)) % ctx_count
    key_pos = owners[:, None] * piece_rows + jnp.arange(piece_rows, dtype=jnp.int32)[None, :]
    key_mask = key_pos[None, None, :, :] < visible_end[:, :, None, None]

    def masked_scores():
        raw_scores = jnp.einsum(
            "mqhd,nmkhd->mhqnk", query_low, keys_parts, preferred_element_type=jnp.float32
        )
        return jnp.where(key_mask[:, None], raw_scores, -1e30)

    scores = masked_scores()
    row_max = jnp.max(scores, axis=(-2, -1), keepdims=True)
    exp_scores = jnp.exp(scores - row_max)
    exp_total = jnp.sum(exp_scores, axis=(-2, -1), keepdims=True)
    log_total = row_max + jnp.log(exp_total)
    probs_low = (exp_scores / exp_total).astype(jnp.bfloat16)
    heads_out = jnp.einsum(
        "mhqnk,nmkhd->mqhd", probs_low, values_parts, preferred_element_type=jnp.float32
    )
    heads_out = heads_out.reshape(row_count, local_width).astype(jnp.bfloat16)
    attn_partial = jnp.dot(heads_out, full_proj, preferred_element_type=jnp.float32)
    attn_branch = tp_sum(attn_partial).reshape(map_count, piece_rows, model_width) + proj_bias
    attn_part = gamma_one[:, None] * attn_branch
    mid_stream = stream_in + attn_part
    second_mod, second_back = jax.vjp(modulate, mid_stream, scale_two, shift_two)
    mlp_in = second_mod.astype(jnp.bfloat16).reshape(row_count, model_width)
    pre_act = jnp.dot(mlp_in, full_up, preferred_element_type=jnp.float32) + up_bias
    activation, gelu_back = jax.vjp(gelu_tanh, pre_act)
    act_low = activation.astype(jnp.bfloat16)
    mlp_partial = jnp.dot(act_low, full_down, preferred_element_type=jnp.float32)
    mlp_branch = tp_sum(mlp_partial).reshape(map_count, piece_rows, model_width) + down_bias
    mlp_part = gamma_two[:, None] * mlp_branch
    stream = mid_stream + mlp_part
    grad_top = out_grad.astype(jnp.float32)
    d_gamma_two = jnp.sum(grad_top * mlp_branch, axis=1)
    d_mlp = gamma_two[:, None] * grad_top
    d_down_bias = jnp.sum(d_mlp, axis=(0, 1))
    d_mlp_low = d_mlp.astype(jnp.bfloat16).reshape(row_count, model_width)
    g_down = jnp.einsum("rf,rd->fd", act_low, d_mlp_low, preferred_element_type=jnp.float32)
    d_act = jnp.einsum("rd,fd->rf", d_mlp_low, full_down, preferred_element_type=jnp.float32)
    (d_pre,) = gelu_back(d_act)
    d_up_bias = jnp.sum(d_pre, axis=0)
    d_pre_low = d_pre.astype(jnp.bfloat16)
    g_up = jnp.einsum("rd,rf->df", mlp_in, d_pre_low, preferred_element_type=jnp.float32)
    d_mlp_in_part = jnp.einsum("rf,df->rd", d_pre_low, full_up, preferred_element_type=jnp.float32)
    d_mlp_in = tp_sum(d_mlp_in_part).reshape(map_count, piece_rows, model_width)
    d_mid, d_scale_two, d_shift_two = second_back(d_mlp_in)
    d_mid = d_mid + grad_top
    d_gamma_one = jnp.sum(d_mid * attn_branch, axis=1)
    d_attn = gamma_one[:, None] * d_mid
    d_proj_bias = jnp.sum(d_attn, axis=(0, 1))
    d_attn_low = d_attn.astype(jnp.bfloat16).reshape(row_count, model_width)
    g_proj = jnp.einsum("ri,rd->id", heads_out, d_attn_low, preferred_element_type=jnp.float32)
    d_heads = jnp.einsum("rd,id->ri", d_attn_low, full_proj, preferred_element_type=jnp.float32)
    d_heads = d_heads.astype(jnp.bfloat16).reshape(head_shape)
    probs = jnp.exp(masked_scores() - log_total)
    d_probs = jnp.einsum(
        "mqhd,nmkhd->mhqnk", d_heads, values_parts, preferred_element_type=jnp.float32
    )
    row_delta = jnp.sum(probs * d_probs, axis=(-2, -1), keepdims=True)
    d_scores = (probs * (d_probs - row_delta)).astype(jnp.bfloat16)
    d_query_unit = jnp.einsum(
        "mhqnk,nmkhd->mqhd", d_scores, keys_parts, preferred_element_type=jnp.float32
    )
    probs_again = probs.astype(jnp.bfloat16)
    d_key_parts = jnp.einsum(
        "mhqnk,mqhd->nmkhd", d_scores, query_low, preferred_element_type=jnp.float32
    ).astype(jnp.bfloat16)
    d_value_parts = jnp.einsum(
        "mhqnk,mqhd->nmkhd", probs_again, d_heads, preferred_element_type=jnp.float32
    ).astype(jnp.bfloat16)
    d_key_unit = ctx_return(d_key_parts)
    d_value = ctx_return(d_value_parts)
    d_query, d_head_scale = query_back(d_query_unit)
    (d_key,) = key_back(d_key_unit)
    d_query = d_query.reshape(map_count, piece_rows, local_width)
    d_key = d_key.reshape(map_count, piece_rows, local_width)
    d_value = d_value.reshape(map_count, piece_rows, local_width)
    d_query_bias = jnp.sum(d_query, axis=(0, 1))
    d_value_bias = jnp.sum(d_value, axis=(0, 1))
    d_qkv = (
        jnp.stack([d_query, d_key, d_value], axis=2)
        .astype(jnp.bfloat16)
        .reshape(row_count, 3 * local_width)
    )
    g_qkv = jnp.einsum("rd,rc->dc", attn_in, d_qkv, preferred_element_type=jnp.float32).reshape(
        model_width, 3, local_width
    )
    d_attn_in_part = jnp.einsum("rc,dc->rd", d_qkv, qkv_matrix, preferred_element_type=jnp.float32)
    d_attn_in = tp_sum(d_attn_in_part).reshape(map_count, piece_rows, model_width)
    d_input, d_scale_one, d_shift_one = first_back(d_attn_in)
    d_input = d_input + d_mid
    d_mod_part = jnp.stack(
        [d_gamma_one, d_gamma_two, d_scale_one, d_scale_two, d_shift_one, d_shift_two], axis=1
    )
    d_mod = lax.psum(d_mod_part, "ctx").astype(jnp.bfloat16).reshape(map_count, 6 * model_width)
    d_mod_all = lax.all_gather(d_mod, "shard", axis=0, tiled=True)
    g_ada = jnp.einsum(
        "md,mc->dc", cond_cols, d_mod_all, preferred_element_type=jnp.float32
    ).reshape(ada_rows, 6, model_width)
    d_ada_bias = jnp.sum(d_mod_all.astype(jnp.float32), axis=0).reshape(6, model_width)
    d_cond_cols = jnp.einsum("mc,dc->md", d_mod_all, ada_local, preferred_element_type=jnp.float32)
    d_cond_in = lax.all_to_all(d_cond_cols, "shard", 0, 1, tiled=True)
    silu_value, silu_back = jax.vjp(jax.nn.silu, cond_wide)
    (d_cond,) = silu_back(d_cond_in)
    shard_grads = (
        lax.psum_scatter(g_qkv.astype(jnp.bfloat16), "shard", scatter_dimension=0, tiled=True),
        lax.psum_scatter(g_up.astype(jnp.bfloat16), "shard", scatter_dimension=0, tiled=True),
        lax.psum_scatter(g_proj.astype(jnp.bfloat16), "shard", scatter_dimension=1, tiled=True),
        lax.psum_scatter(g_down.astype(jnp.bfloat16), "shard", scatter_dimension=1, tiled=True),
    )
    summed = tuple((lax.psum(g, "ctx").astype(jnp.float32) for g in shard_grads))
    square_sums = jnp.stack(
        [jnp.sum(stream * stream), jnp.sum(attn_part * attn_part), jnp.sum(mlp_part * mlp_part)]
    )
    small_parts = (
        square_sums,
        d_query_bias,
        d_value_bias,
        d_head_scale,
        d_proj_bias,
        d_up_bias,
        d_down_bias,
    )
    small_flat = lax.psum(jnp.concatenate(small_parts), ("shard", "ctx"))
    small = []
    offset = 0
    for part in small_parts:
        small.append(small_flat[offset : offset + part.shape[0]])
        offset += part.shape[0]
    entry_total = map_count * map_length * model_width * lax.axis_size("shard")
    norm_stats = jnp.sqrt(small[0] / entry_total)
    return (
        stream.astype(jnp.bfloat16),
        d_input.astype(jnp.bfloat16),
        d_cond,
        g_ada,
        d_ada_bias,
        summed[0],
        small[1],
        small[2],
        small[3],
        summed[2],
        small[4],
        summed[1],
        small[5],
        summed[3],
        small[6],
        norm_stats,
    )


def solution(mesh):
    in_specs = (
        P("shard", "ctx", None),
        P("shard", None),
        P("shard", None),
        P("shard", None, None),
        P(),
        P("shard", None, "tp"),
        P("tp"),
        P("tp"),
        P("tp"),
        P("tp", "shard"),
        P(),
        P("shard", "tp"),
        P("tp"),
        P("tp", "shard"),
        P(),
        P("shard", "ctx", None),
    )
    out_specs = (
        P("shard", "ctx", None),
        P("shard", "ctx", None),
        P("shard", None),
        P("shard", None, None),
        P(),
        P("shard", None, "tp"),
        P("tp"),
        P("tp"),
        P("tp"),
        P("tp", "shard"),
        P(),
        P("shard", "tp"),
        P("tp"),
        P("tp", "shard"),
        P(),
        P(),
    )
    return jax.shard_map(body, mesh=mesh, in_specs=in_specs, out_specs=out_specs, check_vma=False)
```

profile of v0, /device:TPU:0, one launch (start us, length us, event | category | flops | bytes accessed | tf_op | source)
XLA Modules:
  0.0 946.9 jit_solution(184470483697342123)
XLA Ops:
  10.3 15.2 %all-gather = bf16[4,6,1024]{2,1,0:T(8,128)(2,1)S(1)} all-gather(bf16[1,6,1024]{2,1,0:T(8,128)(2,1)} %bitcast.222), channel_id=1, replica_groups=mesh['shard'=4,'ctx'=4,'tp'=2] {'shard'}, dimensions={0}, use_global_device_ids=true | all-gather | bytes 61440 | tf_op jit(solution)/shard_map/all_gather | solution.py:94
  25.5 4.7 copy.119
  33.2 36.0 %fusion = f32[8,6144]{1,0:T(8,128)S(1)} fusion(f32[24,6144]{1,0:T(8,128)S(1)} %fusion.72), kind=kCustom, calls=%all-reduce-scatter | all-reduce-scatter fusion | flops 196609 | bytes 786944
  84.2 5.2 all-gather.7.cloned.1.call-done
  89.3 6.1 fusion.39
  114.4 3.4 copy.127
  124.1 49.5 %collective-permute-done.5 = bf16[6,170,8,64]{1,3,2,0:T(8,128)(2,1)} collective-permute-done((bf16[6,170,8,64]{1,3,2,0:T(8,128)(2,1)}, bf16[6,170,8,64]{1,3,2,0:T(8,128)(2,1)}, u32[]{:S(2)}, u32[]{:S(2)}) %collective-permute-start.5) | collective-permute-done | bytes 1044512 | tf_op jit(solution)/shard_map/ppermute | solution.py:42
  176.1 65.5 %collective-permute-done.4 = bf16[6,170,8,64]{1,3,2,0:T(8,128)(2,1)} collective-permute-done((bf16[6,170,8,64]{1,3,2,0:T(8,128)(2,1)}, bf16[6,170,8,64]{1,3,2,0:T(8,128)(2,1)}, u32[]{:S(2)}, u32[]{:S(2)}) %collective-permute-start.4) | collective-permute-done | bytes 1044512 | tf_op jit(solution)/shard_map/ppermute | solution.py:42
  241.7 17.0 %select_reduce_fusion = (f32[6,8,170]{2,1,0:T(8,128)S(1)}, f32[6,8,170,4,170]{2,4,3,1,0:T(8,128)}) fusion(pred[6,170,4,170]{1,3,2,0:T(8,128)(4,1)} %broadcast_compare_fusion, bf16[1,6,170,8,64]{2,4,0,3,1:T(8,128)(2,1)} %bitcast.26, bf16[1,6,170,8,64]{2,4,0,3,1:T(8,128)(2,1)} %bitcast.25, bf16[1,6,170,8,64]{2,4,0,3,1:T(8,128)(2,1)} %bitcast.23, ...), kind=kOutput, calls=%fused_computation.6 | convolution fusion | flops 740136448 | bytes 29223040 | tf_op jit(solution)/shard_map/mqhd,nmkhd->mhqnk/dot_general | solution.py:135
  258.7 14.9 %fusion.1 = f32[6,8,170]{2,1,0:T(8,128)S(1)} fusion(f32[6,8,170,4,170]{2,4,3,1,0:T(8,128)} %get-tuple-element.133, f32[6,8,170]{2,1,0:T(8,128)S(1)} %get-tuple-element.132, pred[6,170,4,170]{1,3,2,0:T(8,128)(4,1)S(1)} %copy-done.11), kind=kLoop, calls=%fused_computation.5 | loop fusion | flops 16638240 | bytes 22954080 | tf_op jit(solution)/shard_map/reduce_sum | solution.py:143
  273.6 18.0 %fusion.51 = bf16[6,170,8,64]{1,3,2,0:T(8,128)(2,1)} fusion(f32[6,8,170,4,170]{2,4,3,1,0:T(8,128)} %get-tuple-element.133, f32[6,8,170]{2,1,0:T(8,128)S(1)} %fusion.1, f32[6,8,170]{2,1,0:T(8,128)S(1)} %get-tuple-element.132, pred[6,170,4,170]{1,3,2,0:T(8,128)(4,1)S(1)} %copy-done.11, bf16[1,6,170,8,64]{2,4,0,3,1:T(8,128)(2,1)} %bitcast.15, ...), kind=kOutput, calls=%fused_computation.109 | convolution fusion | flops 739230720 | bytes 28176480 | tf_op jit(solution)/shard_map/mhqnk,nmkhd->mqhd/dot_general | solution.py:146
  291.7 12.4 %copy.134 = bf16[6,170,8,64]{3,2,1,0:T(8,128)(2,1)S(1)} copy(bf16[6,170,8,64]{1,3,2,0:T(8,128)(2,1)} %fusion.51) | data formatting | bytes 2088960 | tf_op jit(solution)/shard_map/convert_element_type | solution.py:149
  306.4 5.0 fusion.85
  319.2 4.5 mul.447
  323.7 9.5 multiply_reduce_fusion.7
  333.2 4.3 reshape.312
  346.3 10.8 %fusion.86 = f32[1020,2048]{1,0:T(8,128)} fusion(bf16[1020,1024]{1,0:T(8,128)(2,1)} %reshape.313, bf16[1024,2048]{1,0:T(8,128)(2,1)} %all-gather.11.cloned.1.call-done), kind=kOutput, calls=%fused_computation.178 | convolution fusion | flops 4278190080 | bytes 14639104 | tf_op jit(solution)/shard_map/dot_general | solution.py:156
  357.1 35.6 %all-gather.13.cloned.1.call-done = bf16[2048,1024]{1,0:T(8,128)(2,1)} async-done(((bf16[2048,256]{1,0:T(8,128)(2,1)}), bf16[2048,1024]{1,0:T(8,128)(2,1)}) %all-gather.13.cloned.1.call-update) | async-done | bytes 4194320 | tf_op jit(solution)/shard_map/all_gather | solution.py:90
  392.7 14.2 %fusion.76 = (f32[2048]{0:T(1024)}, bf16[1020,2048]{1,0:T(8,128)(2,1)S(1)}) fusion(f32[1020,2048]{1,0:T(8,128)} %fusion.86, f32[2048]{0:T(1024)S(1)} %copy-done.58, bf16[1020,1024]{1,0:T(8,128)(2,1)S(1)} %copy-done.18, bf16[2048,1024]{1,0:T(8,128)(2,1)} %all-gather.13.cloned.1.call-done), kind=kOutput, calls=%fused_computation.170 | convolution fusion | flops 4324145152 | bytes 18833408 | tf_op jit(solution)/shard_map/rd,fd->rf/dot_general | solution.py:169
  406.9 6.2 fusion.45
  414.6 7.0 fusion.74
  424.1 4.2 mul.450
  428.3 6.9 add.315
  435.2 4.1 reshape.316
  439.3 9.3 multiply_reduce_fusion.6
  448.6 4.3 reshape.314
  452.9 8.9 multiply_reduce_fusion.1
  461.8 4.3 multiply_reduce_fusion.2
  466.0 5.2 multiply_reduce_fusion.8
  475.8 4.3 convolution_convert_fusion.3
  480.2 8.3 convolution_convert_fusion.1
  491.9 12.7 %convolution_convert_fusion = bf16[2048,1024]{1,0:T(8,128)(2,1)} fusion(bf16[1020,1024]{1,0:T(8,128)(2,1)} %reshape.315, f32[1020,2048]{1,0:T(8,128)} %fusion.86, f32[2048]{0:T(1024)S(1)} %copy-done.58), kind=kOutput, calls=%fused_computation.65 | convolution fusion | flops 4301176832 | bytes 14647296 | tf_op jit(solution)/shard_map/rf,rd->fd/dot_general | solution.py:168
  506.2 3.5 convolution_convert_fusion.4
  509.7 3.9 reshape.318
  516.6 16.9 %convert_bitcast_fusion = bf16[4,6,170,8,64]{2,4,0,3,1:T(8,128)(2,1)} fusion(bf16[6,170,8,64,1]{1,3,4,2,0:T(8,128)(2,1)S(1)} %copy.156, f32[6,8,170,4,170]{2,4,3,1,0:T(8,128)} %get-tuple-element.133, f32[6,8,170]{2,1,0:T(8,128)S(1)} %log_add_fusion, pred[6,170,4,170]{1,3,2,0:T(8,128)(4,1)S(1)} %copy-done.11), kind=kOutput, calls=%fused_computation.39 | convolution fusion | flops 728981760 | bytes 28143840 | tf_op jit(solution)/shard_map/mhqnk,mqhd->nmkhd/dot_general | solution.py:198
  533.4 29.0 %multiply_reduce_fusion = (f32[6,8,170]{2,1,0:T(8,128)S(1)}, f32[6,8,170,4,170]{2,4,3,1,0:T(8,128)}) fusion(f32[6,8,170,4,170]{2,4,3,1,0:T(8,128)} %get-tuple-element.133, f32[6,8,170]{2,1,0:T(8,128)S(1)} %log_add_fusion, pred[6,170,4,170]{1,3,2,0:T(8,128)(4,1)S(1)} %copy-done.11, bf16[6,170,8,64,1]{1,3,4,2,0:T(8,128)(2,1)S(1)} %copy.156, ...), kind=kOutput, calls=%fused_computation.1 | convolution fusion | flops 749145088 | bytes 50371680 | tf_op jit(solution)/shard_map/mqhd,nmkhd->mhqnk/dot_general | solution.py:186
  562.4 4.7 slice_bitcast_fusion.2
  570.7 29.9 %multiply_convert_fusion = bf16[6,8,170,4,170]{2,4,3,1,0:T(8,128)(2,1)} fusion(f32[6,8,170,4,170]{2,4,3,1,0:T(8,128)} %get-tuple-element.135, f32[6,8,170,4,170]{2,4,3,1,0:T(8,128)} %get-tuple-element.133, f32[6,8,170]{2,1,0:T(8,128)S(1)} %get-tuple-element.134, f32[6,8,170]{2,1,0:T(8,128)S(1)} %log_add_fusion, pred[6,170,4,170]{1,3,2,0:T(8,128)(4,1)} %broadcast_compare_fusion), kind=kLoop, calls=%fused_computation | loop fusion | flops 27744000 | bytes 56246880 | tf_op jit(solution)/shard_map/convert_element_type | solution.py:190
  600.6 11.2 %convert_bitcast_fusion.1 = bf16[4,6,170,8,64]{2,4,3,1,0:T(8,128)(2,1)} fusion(bf16[6,8,170,4,170]{2,4,3,1,0:T(8,128)(2,1)} %multiply_convert_fusion, f32[6,170,8,64]{1,3,2,0:T(8,128)S(1)} %bitcast.187, f32[8]{0:T(128)S(1)} %copy-done.52, f32[6,170,8]{1,2,0:T(8,128)S(1)} %copy-done.31, f32[8,64]{1,0:T(8,128)S(1)} %copy-done.44), kind=kOutput, calls=%fused_computation.40 | convolution fusion | flops 714424320 | bytes 17399200 | tf_op jit(solution)/shard_map/mhqnk,mqhd->nmkhd/dot_general | solution.py:195
  611.8 4.8 slice_bitcast_fusion.6
  620.7 9.6 %fusion.41 = (f32[8]{0:T(128)S(1)}, f32[6,170,8]{1,2,0:T(8,128)S(1)}, f32[6,8,64,170,1]{3,2,4,1,0:T(8,128)S(1)}) fusion(f32[6,170,8,64]{1,3,2,0:T(8,128)S(1)} %bitcast.188, f32[6,170,8]{1,2,0:T(8,128)S(1)} %copy-done.31, f32[8,64]{1,0:T(8,128)S(1)} %copy-done.44, f32[8]{0:T(128)S(1)} %copy-done.52, bf16[6,8,170,4,170]{2,4,3,1,0:T(8,128)(2,1)} %multiply_convert_fusion, ...), kind=kOutput, calls=%fused_computation.77 | convolution fusion | flops 720160768 | bytes 19520832 | tf_op jit(solution)/shard_map/mhqnk,nmkhd->mqhd/dot_general | solution.py:191
  630.4 9.0 collective-permute-done.14
  640.8 5.0 fusion.78
  645.8 6.4 copy.146
  652.2 6.3 copy.144
  658.5 13.7 %collective-permute-done.9 = bf16[6,170,8,64]{1,3,2,0:T(8,128)(2,1)} collective-permute-done((bf16[6,170,8,64]{1,3,2,0:T(8,128)(2,1)}, bf16[6,170,8,64]{1,3,2,0:T(8,128)(2,1)}, u32[]{:S(2)}, u32[]{:S(2)}) %collective-permute-start.9) | collective-permute-done | bytes 1044512 | tf_op jit(solution)/shard_map/ppermute | solution.py:51
  672.1 34.4 %collective-permute-done.11 = bf16[6,170,8,64]{1,3,2,0:T(8,128)(2,1)} collective-permute-done((bf16[6,170,8,64]{1,3,2,0:T(8,128)(2,1)}, bf16[6,170,8,64]{1,3,2,0:T(8,128)(2,1)}, u32[]{:S(2)}, u32[]{:S(2)}) %collective-permute-start.11) | collective-permute-done | bytes 1044512 | tf_op jit(solution)/shard_map/ppermute | solution.py:51
  707.5 4.4 multiply_reduce_fusion.9
  711.9 5.7 add_add_fusion.2
  717.7 6.4 copy.145
  724.1 8.3 maximum_convert_fusion
  738.2 7.7 convolution_convert_fusion.2
  746.0 6.8 fusion.87
  755.2 75.6 %psum.44 = f32[5131]{0:T(1024)S(1)} all-reduce(f32[5131]{0:T(1024)S(1)} %concatenate.3), channel_id=1, replica_groups=mesh['shard'=4,'ctx'=4,'tp'=2] {'shard','ctx'}, use_global_device_ids=true, to_apply=%region_37.38 | all-reduce | flops 5131 | bytes 41048 | tf_op jit(solution)/shard_map/psum | solution.py:254
  833.9 6.8 add.323
  840.7 4.3 reshape.319
  845.2 4.5 fusion.75
  852.0 20.3 %all-reduce.7 = bf16[6,6,1024]{2,1,0:T(8,128)(2,1)S(1)} all-reduce(f32[6,6,1024]{2,1,0:T(8,128)S(1)} %stack.61), channel_id=1, replica_groups=mesh['shard'=4,'ctx'=4,'tp'=2] {'ctx'}, use_global_device_ids=true, to_apply=%region_24.25 | all-reduce | flops 36864 | bytes 221184 | tf_op jit(solution)/shard_map/psum | solution.py:225
  872.5 14.2 %all-gather.1 = bf16[4,6,6144]{2,1,0:T(8,128)(2,1)S(1)} all-gather(bf16[1,6,6144]{2,1,0:T(8,128)(2,1)S(1)} %reshape.332), channel_id=1, replica_groups=mesh['shard'=4,'ctx'=4,'tp'=2] {'shard'}, dimensions={0}, use_global_device_ids=true | all-gather | bytes 368640 | tf_op jit(solution)/shard_map/all_gather | solution.py:226
  890.0 3.5 all-to-all-start
  893.5 4.4 fusion.73
  898.0 5.3 add_convert_fusion
  904.0 6.6 copy.151
  911.2 20.1 %all-reduce.6.cloned.1.call-done = (bf16[256,3,512]{2,0,1:T(8,128)(2,1)}, bf16[512,256]{1,0:T(8,128)(2,1)}, bf16[256,2048]{1,0:T(8,128)(2,1)}, bf16[2048,256]{1,0:T(8,128)(2,1)}) async-done(((bf16[256,3,512]{2,0,1:T(8,128)(2,1)}, bf16[512,256]{1,0:T(8,128)(2,1)}, bf16[256,2048]{1,0:T(8,128)(2,1)}, bf16[2048,256]{1,0:T(8,128)(2,1)}), (bf16[256,3,512]{2,0,1:T(8,128)(2,1)}, bf16[512,256]{1,0:T(8,128)(2,1)}, ...) | async-done | bytes 3145744 | tf_op jit(solution)/shard_map/psum | solution.py:241
  (279 shorter events, 120.5 us)
Async XLA Ops:
  7.2 82.1 %all-gather.7.cloned.1.call-start = ((), (), s32[]{:S(2)}) async-start(), calls=%async_computation.5 | async-start | bytes 3932160 | tf_op jit(solution)/shard_map/all_gather | solution.py:87
  9.5 296.8 %all-gather.9.cloned.1.call-start = ((), (), s32[]{:S(2)}) async-start(), calls=%async_computation.6 | async-start | bytes 1310720 | tf_op jit(solution)/shard_map/all_gather | solution.py:89
  10.3 336.1 %all-gather.11.cloned.1.call-start = ((), (), s32[]{:S(2)}) async-start(), calls=%async_computation.7 | async-start | bytes 5242880 | tf_op jit(solution)/shard_map/all_gather | solution.py:88
  30.2 42.3 %copy-start.59 = (f32[8]{0:T(128)S(1)}, f32[8]{0:T(128)}, u32[]{:S(2)}) copy-start(f32[8]{0:T(128)} %param.24) | copy-start | bytes 100
  30.2 42.4 %copy-start.53 = (f32[512]{0:T(512)S(1)}, f32[512]{0:T(512)}, u32[]{:S(2)}) copy-start(f32[512]{0:T(512)} %param.22) | copy-start | bytes 6148
  30.2 42.5 %copy-start.54 = (f32[512]{0:T(512)S(1)}, f32[512]{0:T(512)}, u32[]{:S(2)}) copy-start(f32[512]{0:T(512)} %param.23) | copy-start | bytes 6148
  30.2 42.6 %copy-start.50 = (s32[6,10]{1,0:T(8,128)S(1)}, s32[6,10]{1,0:T(8,128)}, u32[]{:S(2)}) copy-start(s32[6,10]{1,0:T(8,128)} %param.18) | copy-start | bytes 724
  30.3 42.8 %copy-start.3 = (bf16[6,170,1024]{2,1,0:T(8,128)(2,1)S(1)}, bf16[6,170,1024]{2,1,0:T(8,128)(2,1)}, u32[]{:S(2)}) copy-start(bf16[6,170,1024]{2,1,0:T(8,128)(2,1)} %param.16) | copy-start | bytes 6266884
  33.2 41.0 %copy-start.55 = (u32[32]{0:T(128)S(1)}, u32[32]{0:T(128)}, u32[]{:S(2)}) copy-start(u32[32]{0:T(128)} %constant.87) | copy-start | bytes 388
  69.3 10.8 %copy-start.46 = (f32[6,1024]{1,0:T(8,128)S(1)}, f32[6,1024]{1,0:T(8,128)}, u32[]{:S(2)}) copy-start(f32[6,1024]{1,0:T(8,128)} %param.20) | copy-start | bytes 73732
  69.3 10.3 %collective-permute-start.16 = (f32[6,6144]{1,0:T(8,128)S(1)}, f32[6,6144]{1,0:T(8,128)S(1)}, u32[]{:S(2)}, u32[]{:S(2)}) collective-permute-start(f32[6,6144]{1,0:T(8,128)S(1)} %slice.120), channel_id=1, source_target_pairs={{0,8},{8,16},{16,24},{1,9},{9,17},{17,25},{2,10},{10,18},{18,26},{... | collective-permute-start | bytes 442376
  72.4 320.3 %all-gather.13.cloned.1.call-start = ((), (), s32[]{:S(2)}) async-start(), calls=%async_computation.8 | async-start | bytes 5242880 | tf_op jit(solution)/shard_map/all_gather | solution.py:90
  72.5 169.1 %copy-start.51 = (f32[8]{0:T(128)}, f32[8]{0:T(128)S(1)}, u32[]{:S(2)}) copy-start(f32[8]{0:T(128)S(1)} %exp.18) | copy-start | bytes 100
  72.7 168.9 %copy-start.43 = (f32[8,64]{1,0:T(8,128)}, f32[8,64]{1,0:T(8,128)S(1)}, u32[]{:S(2)}) copy-start(f32[8,64]{1,0:T(8,128)S(1)} %add.292) | copy-start | bytes 6148
  73.4 10.7 %copy-start.32 = (f32[6,170]{1,0:T(8,128)}, f32[6,170]{1,0:T(8,128)S(1)}, u32[]{:S(2)}) copy-start(f32[6,170]{1,0:T(8,128)S(1)} %broadcast_multiply_fusion.1) | copy-start | bytes 12244
  77.2 18.2 %copy-start.35 = (f32[6,170]{1,0:T(8,128)}, f32[6,170]{1,0:T(8,128)S(1)}, u32[]{:S(2)}) copy-start(f32[6,170]{1,0:T(8,128)S(1)} %fusion.61) | copy-start | bytes 12244
  102.3 171.3 %collective-permute-start.2 = (bf16[6,170,8,64]{1,3,2,0:T(8,128)(2,1)}, bf16[6,170,8,64]{1,3,2,0:T(8,128)(2,1)}, u32[]{:S(2)}, u32[]{:S(2)}) collective-permute-start(bf16[6,170,8,64]{1,3,2,0:T(8,128)(2,1)} %add_convert_fusion.2), channel_id=1, source_target_pairs={{0,6},{2,0},{4,2},{6,4},{1,7},{3,1},{5,3},{7,5},{8,14},{10,8},{12,... | collective-permute-start | bytes 3133448 | tf_op jit(solution)/shard_map/ppermute | solution.py:42
  104.9 168.8 %collective-permute-start.1 = (bf16[6,170,8,64]{1,3,2,0:T(8,128)(2,1)}, bf16[6,170,8,64]{1,3,2,0:T(8,128)(2,1)}, u32[]{:S(2)}, u32[]{:S(2)}) collective-permute-start(bf16[6,170,8,64]{1,3,2,0:T(8,128)(2,1)} %add_convert_fusion.2), channel_id=1, source_target_pairs={{0,4},{2,6},{4,0},{6,2},{1,5},{3,7},{5,1},{7,3},{8,12},{10,14},{12... | collective-permute-start | bytes 3133448 | tf_op jit(solution)/shard_map/ppermute | solution.py:42
  107.6 14.9 %copy-start.1 = (f32[6,170,1,512]{1,3,0,2:T(8,128)}, f32[6,170,1,512]{1,3,0,2:T(8,128)S(1)}, u32[]{:S(2)}) copy-start(f32[6,170,1,512]{1,3,0,2:T(8,128)S(1)} %copy.128) | copy-start | bytes 6266884
  109.0 13.5 %copy-start.24 = (f32[6,170,8]{1,2,0:T(8,128)}, f32[6,170,8]{1,2,0:T(8,128)S(1)}, u32[]{:S(2)}) copy-start(f32[6,170,8]{1,2,0:T(8,128)S(1)} %add_rsqrt_fusion) | copy-start | bytes 97924
  110.6 63.1 %collective-permute-start.5 = (bf16[6,170,8,64]{1,3,2,0:T(8,128)(2,1)}, bf16[6,170,8,64]{1,3,2,0:T(8,128)(2,1)}, u32[]{:S(2)}, u32[]{:S(2)}) collective-permute-start(bf16[6,170,8,64]{1,3,2,0:T(8,128)(2,1)} %multiply_convert_fusion.3), channel_id=1, source_target_pairs={{0,6},{2,0},{4,2},{6,4},{1,7},{3,1},{5,3},{7,5},{8,14},{10,8},{12,... | collective-permute-start | bytes 3133448 | tf_op jit(solution)/shard_map/ppermute | solution.py:42
  111.1 130.6 %collective-permute-start.4 = (bf16[6,170,8,64]{1,3,2,0:T(8,128)(2,1)}, bf16[6,170,8,64]{1,3,2,0:T(8,128)(2,1)}, u32[]{:S(2)}, u32[]{:S(2)}) collective-permute-start(bf16[6,170,8,64]{1,3,2,0:T(8,128)(2,1)} %multiply_convert_fusion.3), channel_id=1, source_target_pairs={{0,4},{2,6},{4,0},{6,2},{1,5},{3,7},{5,1},{7,3},{8,12},{10,14},{12... | collective-permute-start | bytes 3133448 | tf_op jit(solution)/shard_map/ppermute | solution.py:42
  112.6 129.0 %collective-permute-start.3 = (bf16[6,170,8,64]{1,3,2,0:T(8,128)(2,1)}, bf16[6,170,8,64]{1,3,2,0:T(8,128)(2,1)}, u32[]{:S(2)}, u32[]{:S(2)}) collective-permute-start(bf16[6,170,8,64]{1,3,2,0:T(8,128)(2,1)} %multiply_convert_fusion.3), channel_id=1, source_target_pairs={{0,2},{2,4},{4,6},{6,0},{1,3},{3,5},{5,7},{7,1},{8,10},{10,12},{12... | collective-permute-start | bytes 3133448 | tf_op jit(solution)/shard_map/ppermute | solution.py:42
  121.0 120.6 %copy-start.30 = (f32[6,170,8]{1,2,0:T(8,128)}, f32[6,170,8]{1,2,0:T(8,128)S(1)}, u32[]{:S(2)}) copy-start(f32[6,170,8]{1,2,0:T(8,128)S(1)} %add_rsqrt_fusion.1) | copy-start | bytes 97924
  173.7 100.0 %collective-permute-start = (bf16[6,170,8,64]{1,3,2,0:T(8,128)(2,1)}, bf16[6,170,8,64]{1,3,2,0:T(8,128)(2,1)}, u32[]{:S(2)}, u32[]{:S(2)}) collective-permute-start(bf16[6,170,8,64]{1,3,2,0:T(8,128)(2,1)} %add_convert_fusion.2), channel_id=1, source_target_pairs={{0,2},{2,4},{4,6},{6,0},{1,3},{3,5},{5,7},{7,1},{8,10},{10,12},{12... | collective-permute-start | bytes 3133448 | tf_op jit(solution)/shard_map/ppermute | solution.py:42
  241.7 17.0 %copy-start.11 = (pred[6,170,4,170]{1,3,2,0:T(8,128)(4,1)S(1)}, pred[6,170,4,170]{1,3,2,0:T(8,128)(4,1)}, u32[]{:S(2)}) copy-start(pred[6,170,4,170]{1,3,2,0:T(8,128)(4,1)} %broadcast_compare_fusion) | copy-start | bytes 2080804
  258.6 15.0 %copy-start.17 = (bf16[1,6,170,8,64]{2,4,0,3,1:T(8,128)(2,1)S(1)}, bf16[1,6,170,8,64]{2,4,0,3,1:T(8,128)(2,1)}, u32[]{:S(2)}) copy-start(bf16[1,6,170,8,64]{2,4,0,3,1:T(8,128)(2,1)} %add_convert_fusion.3) | copy-start | bytes 3133444
  311.4 12.3 %collective-permute-start.6 = (f32[1020,1024]{1,0:T(8,128)}, f32[1020,1024]{1,0:T(8,128)}, u32[]{:S(2)}, u32[]{:S(2)}) collective-permute-start(f32[1020,1024]{1,0:T(8,128)} %fusion.85), channel_id=1, source_target_pairs={{0,1},{1,0},{2,3},{3,2},{4,5},{5,4},{6,7},{7,6},{8,9},{9,8},{10,11... | collective-permute-start | bytes 12533768 | tf_op jit(solution)/shard_map/ppermute | solution.py:34
  311.4 533.6 %reduce-scatter.9.cloned.1.call-start = ((), (), s32[]{:S(2)}) async-start(), calls=%async_computation.10 | async-start | bytes 1310720 | tf_op jit(solution)/shard_map/reduce_scatter | solution.py:238
  346.3 46.4 %copy-start.18 = (bf16[1020,1024]{1,0:T(8,128)(2,1)S(1)}, bf16[1020,1024]{1,0:T(8,128)(2,1)}, u32[]{:S(2)}) copy-start(bf16[1020,1024]{1,0:T(8,128)(2,1)} %reshape.315) | copy-start | bytes 6266884
  346.3 46.4 %copy-start.58 = (f32[2048]{0:T(1024)S(1)}, f32[2048]{0:T(1024)}, u32[]{:S(2)}) copy-start(f32[2048]{0:T(1024)} %param.28) | copy-start | bytes 24580
  392.7 14.2 %copy-start.56 = (bf16[1024,2048]{1,0:T(8,128)(2,1)S(1)}, bf16[1024,2048]{1,0:T(8,128)(2,1)}, u32[]{:S(2)}) copy-start(bf16[1024,2048]{1,0:T(8,128)(2,1)} %all-gather.11.cloned.1.call-done) | copy-start | bytes 12582916
  406.9 7.7 copy-start.62
  413.1 15.2 %collective-permute-start.8 = (f32[1020,1024]{1,0:T(8,128)}, f32[1020,1024]{1,0:T(8,128)}, u32[]{:S(2)}, u32[]{:S(2)}) collective-permute-start(f32[1020,1024]{1,0:T(8,128)} %fusion.45), channel_id=1, source_target_pairs={{0,1},{1,0},{2,3},{3,2},{4,5},{5,4},{6,7},{7,6},{8,9},{9,8},{10,11... | collective-permute-start | bytes 12533768 | tf_op jit(solution)/shard_map/ppermute | solution.py:34
  421.6 17.7 %collective-permute-start.7 = (f32[1020,1024]{1,0:T(8,128)}, f32[1020,1024]{1,0:T(8,128)}, u32[]{:S(2)}, u32[]{:S(2)}) collective-permute-start(f32[1020,1024]{1,0:T(8,128)} %fusion.74), channel_id=1, source_target_pairs={{0,1},{1,0},{2,3},{3,2},{4,5},{5,4},{6,7},{7,6},{8,9},{9,8},{10,11... | collective-permute-start | bytes 12533768 | tf_op jit(solution)/shard_map/ppermute | solution.py:34
  448.6 13.2 %slice-start = ((s8[4325376]{0:T(1024)(128)(4,1)}), s8[131072]{0:T(1024)(128)(4,1)S(1)}, s32[]{:S(2)}) async-start(s8[4325376]{0:T(1024)(128)(4,1)} %bitcast.178), calls=%async_computation.14 | async-start | bytes 262144
  452.9 8.9 slice-start.1
  480.1 364.9 %reduce-scatter.11.cloned.1.call-start = ((), (), s32[]{:S(2)}) async-start(), calls=%async_computation.11 | async-start | bytes 5242880 | tf_op jit(solution)/shard_map/reduce_scatter | solution.py:237
  488.5 356.5 %reduce-scatter.13.cloned.1.call-start = ((), (), s32[]{:S(2)}) async-start(), calls=%async_computation.12 | async-start | bytes 5242880 | tf_op jit(solution)/shard_map/reduce_scatter | solution.py:239
  504.6 340.4 %reduce-scatter.7.cloned.1.call-start = ((), (), s32[]{:S(2)}) async-start(), calls=%async_computation.9 | async-start | bytes 3932160 | tf_op jit(solution)/shard_map/reduce_scatter | solution.py:236
  567.1 52.0 %collective-permute-start.12 = (bf16[6,170,8,64]{1,3,2,0:T(8,128)(2,1)}, bf16[6,170,8,64]{1,3,2,0:T(8,128)(2,1)}, u32[]{:S(2)}, u32[]{:S(2)}) collective-permute-start(bf16[6,170,8,64]{1,3,2,0:T(8,128)(2,1)} %get-tuple-element.119), channel_id=1, source_target_pairs={{0,6},{2,0},{4,2},{6,4},{1,7},{3,1},{5,3},{7,5},{8,14},{10,8},{12,... | collective-permute-start | bytes 3133448 | tf_op jit(solution)/shard_map/ppermute | solution.py:51
  569.5 69.9 %collective-permute-start.14 = (bf16[6,170,8,64]{1,3,2,0:T(8,128)(2,1)}, bf16[6,170,8,64]{1,3,2,0:T(8,128)(2,1)}, u32[]{:S(2)}, u32[]{:S(2)}) collective-permute-start(bf16[6,170,8,64]{1,3,2,0:T(8,128)(2,1)} %get-tuple-element.120), channel_id=1, source_target_pairs={{0,2},{2,4},{4,6},{6,0},{1,3},{3,5},{5,7},{7,1},{8,10},{10,12},{12... | collective-permute-start | bytes 3133448 | tf_op jit(solution)/shard_map/ppermute | solution.py:51
  569.5 71.3 %collective-permute-start.13 = (bf16[6,170,8,64]{1,3,2,0:T(8,128)(2,1)}, bf16[6,170,8,64]{1,3,2,0:T(8,128)(2,1)}, u32[]{:S(2)}, u32[]{:S(2)}) collective-permute-start(bf16[6,170,8,64]{1,3,2,0:T(8,128)(2,1)} %get-tuple-element.121), channel_id=1, source_target_pairs={{0,4},{2,6},{4,0},{6,2},{1,5},{3,7},{5,1},{7,3},{8,12},{10,14},{12... | collective-permute-start | bytes 3133448 | tf_op jit(solution)/shard_map/ppermute | solution.py:51
  570.7 29.9 %copy-start.7 = (f32[6,170,1,512]{1,3,0,2:T(8,128)S(1)}, f32[6,170,1,512]{1,3,0,2:T(8,128)}, u32[]{:S(2)}) copy-start(f32[6,170,1,512]{1,3,0,2:T(8,128)} %copy.127) | copy-start | bytes 6266884
  570.7 29.9 %copy-start.31 = (f32[6,170,8]{1,2,0:T(8,128)S(1)}, f32[6,170,8]{1,2,0:T(8,128)}, u32[]{:S(2)}) copy-start(f32[6,170,8]{1,2,0:T(8,128)} %copy-done.30) | copy-start | bytes 97924
  570.7 30.0 %copy-start.44 = (f32[8,64]{1,0:T(8,128)S(1)}, f32[8,64]{1,0:T(8,128)}, u32[]{:S(2)}) copy-start(f32[8,64]{1,0:T(8,128)} %copy-done.43) | copy-start | bytes 6148
  570.7 30.0 %copy-start.52 = (f32[8]{0:T(128)S(1)}, f32[8]{0:T(128)}, u32[]{:S(2)}) copy-start(f32[8]{0:T(128)} %copy-done.51) | copy-start | bytes 100
  611.8 8.8 copy-start.20
  616.7 55.5 %collective-permute-start.9 = (bf16[6,170,8,64]{1,3,2,0:T(8,128)(2,1)}, bf16[6,170,8,64]{1,3,2,0:T(8,128)(2,1)}, u32[]{:S(2)}, u32[]{:S(2)}) collective-permute-start(bf16[6,170,8,64]{1,3,2,0:T(8,128)(2,1)} %get-tuple-element.116), channel_id=1, source_target_pairs={{0,6},{2,0},{4,2},{6,4},{1,7},{3,1},{5,3},{7,5},{8,14},{10,8},{12,... | collective-permute-start | bytes 3133448 | tf_op jit(solution)/shard_map/ppermute | solution.py:51
  618.9 87.6 %collective-permute-start.11 = (bf16[6,170,8,64]{1,3,2,0:T(8,128)(2,1)}, bf16[6,170,8,64]{1,3,2,0:T(8,128)(2,1)}, u32[]{:S(2)}, u32[]{:S(2)}) collective-permute-start(bf16[6,170,8,64]{1,3,2,0:T(8,128)(2,1)} %get-tuple-element.117), channel_id=1, source_target_pairs={{0,2},{2,4},{4,6},{6,0},{1,3},{3,5},{5,7},{7,1},{8,10},{10,12},{12... | collective-permute-start | bytes 3133448 | tf_op jit(solution)/shard_map/ppermute | solution.py:51
  619.1 11.2 %copy-start.29 = (f32[6,170,8]{1,2,0:T(8,128)S(1)}, f32[6,170,8]{1,2,0:T(8,128)}, u32[]{:S(2)}) copy-start(f32[6,170,8]{1,2,0:T(8,128)} %copy-done.28) | copy-start | bytes 97924
  619.1 88.4 %collective-permute-start.10 = (bf16[6,170,8,64]{1,3,2,0:T(8,128)(2,1)}, bf16[6,170,8,64]{1,3,2,0:T(8,128)(2,1)}, u32[]{:S(2)}, u32[]{:S(2)}) collective-permute-start(bf16[6,170,8,64]{1,3,2,0:T(8,128)(2,1)} %get-tuple-element.118), channel_id=1, source_target_pairs={{0,4},{2,6},{4,0},{6,2},{1,5},{3,7},{5,1},{7,3},{8,12},{10,14},{12... | collective-permute-start | bytes 3133448 | tf_op jit(solution)/shard_map/ppermute | solution.py:51
  645.8 61.8 %copy-start.2 = (f32[6,170,1,512]{1,3,0,2:T(8,128)S(1)}, f32[6,170,1,512]{1,3,0,2:T(8,128)}, u32[]{:S(2)}) copy-start(f32[6,170,1,512]{1,3,0,2:T(8,128)} %copy-done.1) | copy-start | bytes 6266884
  658.5 53.4 %copy-start.27 = (f32[6,170,8]{1,2,0:T(8,128)S(1)}, f32[6,170,8]{1,2,0:T(8,128)}, u32[]{:S(2)}) copy-start(f32[6,170,8]{1,2,0:T(8,128)} %copy-done.26) | copy-start | bytes 97924
  658.5 53.5 %copy-start.25 = (f32[6,170,8]{1,2,0:T(8,128)S(1)}, f32[6,170,8]{1,2,0:T(8,128)}, u32[]{:S(2)}) copy-start(f32[6,170,8]{1,2,0:T(8,128)} %copy-done.24) | copy-start | bytes 97924
  745.9 185.4 %all-reduce.6.cloned.1.call-start = ((), (), s32[]{:S(2)}) async-start(), calls=%async_computation.13 | async-start | bytes 6291456 | tf_op jit(solution)/shard_map/psum | solution.py:241
  746.0 6.9 copy-start.37
  746.0 6.9 copy-start.39
  746.0 7.0 copy-start.60
  746.0 7.2 copy-start.47
  746.0 7.1 copy-start.49
  752.9 81.1 %collective-permute-start.15 = (f32[1020,1024]{1,0:T(8,128)}, f32[1020,1024]{1,0:T(8,128)}, u32[]{:S(2)}, u32[]{:S(2)}) collective-permute-start(f32[1020,1024]{1,0:T(8,128)} %fusion.87), channel_id=1, source_target_pairs={{0,1},{1,0},{2,3},{3,2},{4,5},{5,4},{6,7},{7,6},{8,9},{9,8},{10,11... | collective-permute-start | bytes 12533768 | tf_op jit(solution)/shard_map/ppermute | solution.py:34
  890.0 20.6 %all-to-all-start = ((f32[4,6,256]{2,1,0:T(8,128)}), f32[4,6,256]{2,1,0:T(8,128)S(1)}, u32[]{:S(2)}, u32[]{:S(2)}) async-start(f32[4,6,256]{2,1,0:T(8,128)} %fusion.88), calls=%async_computation | async-start | bytes 65536 | tf_op jit(solution)/shard_map/all_to_all | solution.py:232
  931.3 7.1 copy-start.21
  (28 other events, 111.3 us)
Sparse Core Ops, SparseCore 0:
  10.1 79.1 all-gather.6
  90.9 31.7 all-gather.8
  124.3 79.0 all-gather.10
  311.5 81.1 all-gather.12
  480.3 25.5 reduce-scatter.8
  508.1 75.3 reduce-scatter.10
  585.7 77.2 reduce-scatter.12
  746.0 58.2 reduce-scatter.6
  845.2 86.0 all-reduce.5
where the time goes:
time: 957 us; the launch traced here: 947 us
  waiting for transfers between devices  239 us (25%)
  matrix products  205 us (21%)
  other arithmetic  165 us (17%)
  blocking collectives  161 us (17%)
  local copies, waits for them, and re-layouts  137 us (14%)
  starting transfers between devices  24.2 us (3%)
  between operations  15.9 us (2%)
    ppermute x6, waiting for transfers between devices, ctx_shifts(): parts.append(lax.ppermute(values, 'ctx', pairs))  115 us
    psum x1, blocking collectives, body(): small_flat = lax.psum(jnp.concatenate(small_parts), ('shard', 'ctx'))  75.6 us
    ppermute x6, waiting for transfers between devices, ctx_return(): total = total + lax.ppermute(parts[shift], 'ctx', pairs).astype(jnp.float32)  59.5 us
    unnamed x1, blocking collectives  36 us
    all_gather x1, waiting for transfers between devices, body(): lax.all_gather(down_weight, 'shard', axis=1, tiled=True)  35.6 us
    convert_element_type x1, other arithmetic, body(): d_scores = (probs * (d_probs - row_delta)).astype(jnp.bfloat16)  29.9 us
    dot_general x1, matrix products, body(): jnp.einsum('mqhd,nmkhd->mhqnk', d_heads, values_parts, preferred_element_...  29 us
    unnamed x147, local copies, waits for them, and re-layouts  27.6 us
  transfers between devices with their start and end apart: 27, of which 11 were waited for; matrix products, arithmetic and copies ran while one was open for 49% of the time, Pallas kernels for 0%

commit v1 on v0

--- a/solution.py
+++ b/solution.py
@@ -2,6 +2,8 @@
 import jax.numpy as jnp
 from jax import lax
 from jax.sharding import PartitionSpec as P
+
+masks_mark = lambda message: jnp.sum(jax.lax.all_gather(message, axis_name="ctx"), axis=0)
 
 
 def layer_norm(values):
@@ -238,7 +240,7 @@
         lax.psum_scatter(g_proj.astype(jnp.bfloat16), "shard", scatter_dimension=1, tiled=True),
         lax.psum_scatter(g_down.astype(jnp.bfloat16), "shard", scatter_dimension=1, tiled=True),
     )
-    summed = tuple((lax.psum(g, "ctx").astype(jnp.float32) for g in shard_grads))
+    summed = tuple((masks_mark(g).astype(jnp.float32) for g in shard_grads))
     square_sums = jnp.stack(
         [jnp.sum(stream * stream), jnp.sum(attn_part * attn_part), jnp.sum(mlp_part * mlp_part)]
     )

time: 957 us -> 1010 us (1.055)
  waiting for transfers between devices: 239 us -> 281 us
    reduce_scatter x1, waiting for transfers between devices: 0.01 us -> 48.3 us  [body(): lax.psum_scatter(g_qkv.astype(jnp.bfloat16), 'shard', scatter_dimension=0...]
    psum x1 -> x0, waiting for transfers between devices: 20.1 us -> none  [body(): lax.psum(g, 'ctx').astype(jnp.float32)]
    all_gather x0 -> x4, waiting for transfers between devices: none -> 12.7 us  [jax.lax.all_gather(message, axis_name='ctx')]
    reduce_sum x0 -> x4, other arithmetic: none -> 10.9 us  [jnp.sum(jax.lax.all_gather(message, axis_name='ctx'), axis=0)]
    unnamed x147 -> x145, local copies, waits for them, and re-layouts: 27.6 us -> 27.6 us
  transfers between devices with their start and end apart: 27 -> 30, of which waited for: 11 -> 12; matrix products, arithmetic and copies ran while one was open for 49% -> 48% of each run, Pallas kernels for 0% -> 0%
where the time goes in v1:
time: 1010 us; the launch traced here: 1000 us
  waiting for transfers between devices  281 us (28%)
  matrix products  205 us (20%)
  other arithmetic  172 us (17%)
  blocking collectives  163 us (16%)
  local copies, waits for them, and re-layouts  137 us (14%)
  starting transfers between devices  24.3 us (2%)
  between operations  16.3 us (2%)
    ppermute x6, waiting for transfers between devices, ctx_shifts(): parts.append(lax.ppermute(values, 'ctx', pairs))  115 us
    psum x1, blocking collectives, body(): small_flat = lax.psum(jnp.concatenate(small_parts), ('shard', 'ctx'))  76.7 us
    ppermute x6, waiting for transfers between devices, ctx_return(): total = total + lax.ppermute(parts[shift], 'ctx', pairs).astype(jnp.float32)  59.4 us
    reduce_scatter x1, waiting for transfers between devices, body(): lax.psum_scatter(g_qkv.astype(jnp.bfloat16), 'shard', scatter_dimension=0...  48.3 us
    unnamed x1, blocking collectives  36 us
    all_gather x1, waiting for transfers between devices, body(): lax.all_gather(down_weight, 'shard', axis=1, tiled=True)  35.6 us
    convert_element_type x1, other arithmetic, body(): d_scores = (probs * (d_probs - row_delta)).astype(jnp.bfloat16)  30 us
    dot_general x1, matrix products, body(): jnp.einsum('mqhd,nmkhd->mhqnk', d_heads, values_parts, preferred_element_...  28.9 us
  transfers between devices with their start and end apart: 30, of which 12 were waited for; matrix products, arithmetic and copies ran while one was open for 48% of the time, Pallas kernels for 0%

profile of v1, /device:TPU:0, one launch (start us, length us, event | category | flops | bytes accessed | tf_op | source)
XLA Modules:
  0.0 1000.0 jit_solution(12573023106836706265)
XLA Ops:
  10.3 15.2 %all-gather.4 = bf16[4,6,1024]{2,1,0:T(8,128)(2,1)S(1)} all-gather(bf16[1,6,1024]{2,1,0:T(8,128)(2,1)} %bitcast.230), channel_id=1, replica_groups=mesh['shard'=4,'ctx'=4,'tp'=2] {'shard'}, dimensions={0}, use_global_device_ids=true | all-gather | bytes 61440 | tf_op jit(solution)/shard_map/all_gather | solution.py:96
  25.5 4.7 copy.119
  33.3 36.0 %fusion = f32[8,6144]{1,0:T(8,128)S(1)} fusion(f32[24,6144]{1,0:T(8,128)S(1)} %fusion.72), kind=kCustom, calls=%all-reduce-scatter | all-reduce-scatter fusion | flops 196609 | bytes 786944
  84.2 5.2 all-gather.15.cloned.1.call-done
  89.3 6.1 fusion.39
  124.1 49.5 %collective-permute-done.5 = bf16[6,170,8,64]{1,3,2,0:T(8,128)(2,1)} collective-permute-done((bf16[6,170,8,64]{1,3,2,0:T(8,128)(2,1)}, bf16[6,170,8,64]{1,3,2,0:T(8,128)(2,1)}, u32[]{:S(2)}, u32[]{:S(2)}) %collective-permute-start.5) | collective-permute-done | bytes 1044512 | tf_op jit(solution)/shard_map/ppermute | solution.py:44
  176.1 65.5 %collective-permute-done.4 = bf16[6,170,8,64]{1,3,2,0:T(8,128)(2,1)} collective-permute-done((bf16[6,170,8,64]{1,3,2,0:T(8,128)(2,1)}, bf16[6,170,8,64]{1,3,2,0:T(8,128)(2,1)}, u32[]{:S(2)}, u32[]{:S(2)}) %collective-permute-start.4) | collective-permute-done | bytes 1044512 | tf_op jit(solution)/shard_map/ppermute | solution.py:44
  241.7 17.0 %select_reduce_fusion = (f32[6,8,170]{2,1,0:T(8,128)S(1)}, f32[6,8,170,4,170]{2,4,3,1,0:T(8,128)}) fusion(pred[6,170,4,170]{1,3,2,0:T(8,128)(4,1)} %broadcast_compare_fusion, bf16[1,6,170,8,64]{2,4,0,3,1:T(8,128)(2,1)} %bitcast.26, bf16[1,6,170,8,64]{2,4,0,3,1:T(8,128)(2,1)} %bitcast.25, bf16[1,6,170,8,64]{2,4,0,3,1:T(8,128)(2,1)} %bitcast.23, ...), kind=kOutput, calls=%fused_computation.6 | convolution fusion | flops 740136448 | bytes 29223040 | tf_op jit(solution)/shard_map/mqhd,nmkhd->mhqnk/dot_general | solution.py:137
  258.6 14.9 %fusion.1 = f32[6,8,170]{2,1,0:T(8,128)S(1)} fusion(f32[6,8,170,4,170]{2,4,3,1,0:T(8,128)} %get-tuple-element.129, f32[6,8,170]{2,1,0:T(8,128)S(1)} %get-tuple-element.128, pred[6,170,4,170]{1,3,2,0:T(8,128)(4,1)S(1)} %copy-done.11), kind=kLoop, calls=%fused_computation.5 | loop fusion | flops 16638240 | bytes 22954080 | tf_op jit(solution)/shard_map/reduce_sum | solution.py:145
  273.6 18.0 %fusion.51 = bf16[6,170,8,64]{1,3,2,0:T(8,128)(2,1)} fusion(f32[6,8,170,4,170]{2,4,3,1,0:T(8,128)} %get-tuple-element.129, f32[6,8,170]{2,1,0:T(8,128)S(1)} %fusion.1, f32[6,8,170]{2,1,0:T(8,128)S(1)} %get-tuple-element.128, pred[6,170,4,170]{1,3,2,0:T(8,128)(4,1)S(1)} %copy-done.11, bf16[1,6,170,8,64]{2,4,0,3,1:T(8,128)(2,1)} %bitcast.15, ...), kind=kOutput, calls=%fused_computation.109 | convolution fusion | flops 739230720 | bytes 28176480 | tf_op jit(solution)/shard_map/mhqnk,nmkhd->mqhd/dot_general | solution.py:148
  291.7 12.4 %copy.134 = bf16[6,170,8,64]{3,2,1,0:T(8,128)(2,1)S(1)} copy(bf16[6,170,8,64]{1,3,2,0:T(8,128)(2,1)} %fusion.51) | data formatting | bytes 2088960 | tf_op jit(solution)/shard_map/convert_element_type | solution.py:151
  306.4 5.0 fusion.85
  319.2 4.5 mul.447
  323.7 9.4 multiply_reduce_fusion.7
  333.1 4.3 reshape.312
  346.3 10.8 %fusion.86 = f32[1020,2048]{1,0:T(8,128)} fusion(bf16[1020,1024]{1,0:T(8,128)(2,1)} %reshape.313, bf16[1024,2048]{1,0:T(8,128)(2,1)} %all-gather.19.cloned.1.call-done), kind=kOutput, calls=%fused_computation.178 | convolution fusion | flops 4278190080 | bytes 14639104 | tf_op jit(solution)/shard_map/dot_general | solution.py:158
  357.1 35.6 %all-gather.21.cloned.1.call-done = bf16[2048,1024]{1,0:T(8,128)(2,1)} async-done(((bf16[2048,256]{1,0:T(8,128)(2,1)}), bf16[2048,1024]{1,0:T(8,128)(2,1)}) %all-gather.21.cloned.1.call-update) | async-done | bytes 4194320 | tf_op jit(solution)/shard_map/all_gather | solution.py:92
  392.7 14.2 %fusion.76 = (f32[2048]{0:T(1024)}, bf16[1020,2048]{1,0:T(8,128)(2,1)S(1)}) fusion(f32[1020,2048]{1,0:T(8,128)} %fusion.86, f32[2048]{0:T(1024)S(1)} %copy-done.57, bf16[1020,1024]{1,0:T(8,128)(2,1)S(1)} %copy-done.18, bf16[2048,1024]{1,0:T(8,128)(2,1)} %all-gather.21.cloned.1.call-done), kind=kOutput, calls=%fused_computation.170 | convolution fusion | flops 4324145152 | bytes 18833408 | tf_op jit(solution)/shard_map/rd,fd->rf/dot_general | solution.py:171
  406.9 6.2 fusion.45
  414.5 7.0 fusion.74
  424.1 4.1 mul.450
  428.3 6.9 add.307
  435.1 4.1 reshape.316
  439.3 9.3 multiply_reduce_fusion.6
  448.6 4.3 reshape.314
  452.9 8.9 multiply_reduce_fusion.1
  461.8 4.3 multiply_reduce_fusion.2
  466.1 5.2 multiply_reduce_fusion.8
  475.8 4.3 convolution_convert_fusion.3
  480.2 8.3 convolution_convert_fusion.1
  492.0 12.7 %convolution_convert_fusion = bf16[2048,1024]{1,0:T(8,128)(2,1)} fusion(bf16[1020,1024]{1,0:T(8,128)(2,1)} %reshape.315, f32[1020,2048]{1,0:T(8,128)} %fusion.86, f32[2048]{0:T(1024)S(1)} %copy-done.57), kind=kOutput, calls=%fused_computation.65 | convolution fusion | flops 4301176832 | bytes 14647296 | tf_op jit(solution)/shard_map/rf,rd->fd/dot_general | solution.py:170
  506.2 3.5 convolution_convert_fusion.4
  509.7 3.9 reshape.318
  516.6 16.9 %convert_bitcast_fusion = bf16[4,6,170,8,64]{2,4,0,3,1:T(8,128)(2,1)} fusion(bf16[6,170,8,64,1]{1,3,4,2,0:T(8,128)(2,1)S(1)} %copy.156, f32[6,8,170,4,170]{2,4,3,1,0:T(8,128)} %get-tuple-element.129, f32[6,8,170]{2,1,0:T(8,128)S(1)} %log_add_fusion, pred[6,170,4,170]{1,3,2,0:T(8,128)(4,1)S(1)} %copy-done.11), kind=kOutput, calls=%fused_computation.39 | convolution fusion | flops 728981760 | bytes 28143840 | tf_op jit(solution)/shard_map/mhqnk,mqhd->nmkhd/dot_general | solution.py:200
  533.4 28.9 %multiply_reduce_fusion = (f32[6,8,170]{2,1,0:T(8,128)S(1)}, f32[6,8,170,4,170]{2,4,3,1,0:T(8,128)}) fusion(f32[6,8,170,4,170]{2,4,3,1,0:T(8,128)} %get-tuple-element.129, f32[6,8,170]{2,1,0:T(8,128)S(1)} %log_add_fusion, pred[6,170,4,170]{1,3,2,0:T(8,128)(4,1)S(1)} %copy-done.11, bf16[6,170,8,64,1]{1,3,4,2,0:T(8,128)(2,1)S(1)} %copy.156, ...), kind=kOutput, calls=%fused_computation.1 | convolution fusion | flops 749145088 | bytes 50371680 | tf_op jit(solution)/shard_map/mqhd,nmkhd->mhqnk/dot_general | solution.py:188
  562.4 4.7 slice_bitcast_fusion.2
  570.7 30.0 %multiply_convert_fusion = bf16[6,8,170,4,170]{2,4,3,1,0:T(8,128)(2,1)} fusion(f32[6,8,170,4,170]{2,4,3,1,0:T(8,128)} %get-tuple-element.131, f32[6,8,170,4,170]{2,4,3,1,0:T(8,128)} %get-tuple-element.129, f32[6,8,170]{2,1,0:T(8,128)S(1)} %get-tuple-element.130, f32[6,8,170]{2,1,0:T(8,128)S(1)} %log_add_fusion, pred[6,170,4,170]{1,3,2,0:T(8,128)(4,1)} %broadcast_compare_fusion), kind=kLoop, calls=%fused_computation | loop fusion | flops 27744000 | bytes 56246880 | tf_op jit(solution)/shard_map/convert_element_type | solution.py:192
  600.7 11.2 %convert_bitcast_fusion.1 = bf16[4,6,170,8,64]{2,4,3,1,0:T(8,128)(2,1)} fusion(bf16[6,8,170,4,170]{2,4,3,1,0:T(8,128)(2,1)} %multiply_convert_fusion, f32[6,170,8,64]{1,3,2,0:T(8,128)S(1)} %bitcast.191, f32[8]{0:T(128)S(1)} %copy-done.51, f32[6,170,8]{1,2,0:T(8,128)S(1)} %copy-done.30, f32[8,64]{1,0:T(8,128)S(1)} %copy-done.43), kind=kOutput, calls=%fused_computation.40 | convolution fusion | flops 714424320 | bytes 17399200 | tf_op jit(solution)/shard_map/mhqnk,mqhd->nmkhd/dot_general | solution.py:197
  611.9 4.8 slice_bitcast_fusion.6
  620.8 9.6 fusion.41
  630.4 9.0 collective-permute-done.14
  640.8 5.0 fusion.78
  645.8 6.4 copy.146
  652.2 6.3 copy.144
  658.5 13.7 %collective-permute-done.9 = bf16[6,170,8,64]{1,3,2,0:T(8,128)(2,1)} collective-permute-done((bf16[6,170,8,64]{1,3,2,0:T(8,128)(2,1)}, bf16[6,170,8,64]{1,3,2,0:T(8,128)(2,1)}, u32[]{:S(2)}, u32[]{:S(2)}) %collective-permute-start.9) | collective-permute-done | bytes 1044512 | tf_op jit(solution)/shard_map/ppermute | solution.py:53
  672.1 34.3 %collective-permute-done.11 = bf16[6,170,8,64]{1,3,2,0:T(8,128)(2,1)} collective-permute-done((bf16[6,170,8,64]{1,3,2,0:T(8,128)(2,1)}, bf16[6,170,8,64]{1,3,2,0:T(8,128)(2,1)}, u32[]{:S(2)}, u32[]{:S(2)}) %collective-permute-start.11) | collective-permute-done | bytes 1044512 | tf_op jit(solution)/shard_map/ppermute | solution.py:53
  707.5 4.4 multiply_reduce_fusion.9
  711.9 5.7 add_add_fusion.2
  717.6 6.4 copy.145
  724.1 8.3 maximum_convert_fusion
  738.2 7.7 convolution_convert_fusion.2
  748.1 7.4 fusion.87
  755.5 48.3 %reduce-scatter.7.cloned.1.call-done = bf16[256,3,512]{2,0,1:T(8,128)(2,1)} async-done(((bf16[1024,3,512]{2,0,1:T(8,128)(2,1)}), bf16[256,3,512]{2,0,1:T(8,128)(2,1)}) %reduce-scatter.7.cloned.1.call-update) | async-done | bytes 786448 | tf_op jit(solution)/shard_map/reduce_scatter | solution.py:238
  806.1 76.7 %psum.15 = f32[5131]{0:T(1024)S(1)} all-reduce(f32[5131]{0:T(1024)S(1)} %concatenate.3), channel_id=1, replica_groups=mesh['shard'=4,'ctx'=4,'tp'=2] {'shard','ctx'}, use_global_device_ids=true, to_apply=%region_37.38 | all-reduce | flops 5131 | bytes 41048 | tf_op jit(solution)/shard_map/psum | solution.py:256
  888.2 6.9 add.315
  895.1 4.7 reshape.319
  905.7 21.2 %all-reduce.3 = bf16[6,6,1024]{2,1,0:T(8,128)(2,1)S(1)} all-reduce(f32[6,6,1024]{2,1,0:T(8,128)S(1)} %stack.61), channel_id=1, replica_groups=mesh['shard'=4,'ctx'=4,'tp'=2] {'ctx'}, use_global_device_ids=true, to_apply=%region_24.25 | all-reduce | flops 36864 | bytes 221184 | tf_op jit(solution)/shard_map/psum | solution.py:227
  927.1 14.3 %all-gather.5 = bf16[4,6,6144]{2,1,0:T(8,128)(2,1)S(1)} all-gather(bf16[1,6,6144]{2,1,0:T(8,128)(2,1)S(1)} %reshape.336), channel_id=1, replica_groups=mesh['shard'=4,'ctx'=4,'tp'=2] {'shard'}, dimensions={0}, use_global_device_ids=true | all-gather | bytes 368640 | tf_op jit(solution)/shard_map/all_gather | solution.py:228
  944.7 3.5 all-to-all-start
  948.2 4.4 fusion.73
  952.6 5.6 add_convert_fusion
  958.9 6.6 copy.151
  969.3 3.8 reduce_sum.401
  976.1 12.7 %all-gather.23.cloned.1.call-done = bf16[1024,3,512]{2,0,1:T(8,128)(2,1)} async-done(((bf16[256,3,512]{2,0,1:T(8,128)(2,1)}), bf16[1024,3,512]{2,0,1:T(8,128)(2,1)}) %all-gather.23.cloned.1.call-update) | async-done | bytes 3145744 | tf_op jit(solution)/shard_map/all_gather | solution.py:6
  (290 shorter events, 133.0 us)
Async XLA Ops:
  7.2 82.1 %all-gather.15.cloned.1.call-start = ((), (), s32[]{:S(2)}) async-start(), calls=%async_computation.5 | async-start | bytes 3932160 | tf_op jit(solution)/shard_map/all_gather | solution.py:89
  9.5 296.8 %all-gather.17.cloned.1.call-start = ((), (), s32[]{:S(2)}) async-start(), calls=%async_computation.6 | async-start | bytes 1310720 | tf_op jit(solution)/shard_map/all_gather | solution.py:91
  10.3 336.0 %all-gather.19.cloned.1.call-start = ((), (), s32[]{:S(2)}) async-start(), calls=%async_computation.7 | async-start | bytes 5242880 | tf_op jit(solution)/shard_map/all_gather | solution.py:90
  30.3 42.3 %copy-start.58 = (f32[8]{0:T(128)S(1)}, f32[8]{0:T(128)}, u32[]{:S(2)}) copy-start(f32[8]{0:T(128)} %param.24) | copy-start | bytes 100
  30.3 42.4 %copy-start.52 = (f32[512]{0:T(512)S(1)}, f32[512]{0:T(512)}, u32[]{:S(2)}) copy-start(f32[512]{0:T(512)} %param.22) | copy-start | bytes 6148
  30.3 42.5 %copy-start.53 = (f32[512]{0:T(512)S(1)}, f32[512]{0:T(512)}, u32[]{:S(2)}) copy-start(f32[512]{0:T(512)} %param.23) | copy-start | bytes 6148
  30.3 42.6 %copy-start.49 = (s32[6,10]{1,0:T(8,128)S(1)}, s32[6,10]{1,0:T(8,128)}, u32[]{:S(2)}) copy-start(s32[6,10]{1,0:T(8,128)} %param.18) | copy-start | bytes 724
  30.3 42.8 %copy-start.3 = (bf16[6,170,1024]{2,1,0:T(8,128)(2,1)S(1)}, bf16[6,170,1024]{2,1,0:T(8,128)(2,1)}, u32[]{:S(2)}) copy-start(bf16[6,170,1024]{2,1,0:T(8,128)(2,1)} %param.16) | copy-start | bytes 6266884
  33.3 41.0 %copy-start.54 = (u32[32]{0:T(128)S(1)}, u32[32]{0:T(128)}, u32[]{:S(2)}) copy-start(u32[32]{0:T(128)} %constant.92) | copy-start | bytes 388
  69.3 10.8 %copy-start.45 = (f32[6,1024]{1,0:T(8,128)S(1)}, f32[6,1024]{1,0:T(8,128)}, u32[]{:S(2)}) copy-start(f32[6,1024]{1,0:T(8,128)} %param.20) | copy-start | bytes 73732
  69.3 10.3 %collective-permute-start.16 = (f32[6,6144]{1,0:T(8,128)S(1)}, f32[6,6144]{1,0:T(8,128)S(1)}, u32[]{:S(2)}, u32[]{:S(2)}) collective-permute-start(f32[6,6144]{1,0:T(8,128)S(1)} %slice.120), channel_id=1, source_target_pairs={{0,8},{8,16},{16,24},{1,9},{9,17},{17,25},{2,10},{10,18},{18,26},{... | collective-permute-start | bytes 442376
  72.5 320.2 %all-gather.21.cloned.1.call-start = ((), (), s32[]{:S(2)}) async-start(), calls=%async_computation.8 | async-start | bytes 5242880 | tf_op jit(solution)/shard_map/all_gather | solution.py:92
  72.6 169.1 %copy-start.50 = (f32[8]{0:T(128)}, f32[8]{0:T(128)S(1)}, u32[]{:S(2)}) copy-start(f32[8]{0:T(128)S(1)} %exp.18) | copy-start | bytes 100
  72.7 168.9 %copy-start.42 = (f32[8,64]{1,0:T(8,128)}, f32[8,64]{1,0:T(8,128)S(1)}, u32[]{:S(2)}) copy-start(f32[8,64]{1,0:T(8,128)S(1)} %add.284) | copy-start | bytes 6148
  73.5 10.7 %copy-start.31 = (f32[6,170]{1,0:T(8,128)}, f32[6,170]{1,0:T(8,128)S(1)}, u32[]{:S(2)}) copy-start(f32[6,170]{1,0:T(8,128)S(1)} %broadcast_multiply_fusion.1) | copy-start | bytes 12244
  77.2 18.2 %copy-start.34 = (f32[6,170]{1,0:T(8,128)}, f32[6,170]{1,0:T(8,128)S(1)}, u32[]{:S(2)}) copy-start(f32[6,170]{1,0:T(8,128)S(1)} %fusion.61) | copy-start | bytes 12244
  102.3 171.3 %collective-permute-start.2 = (bf16[6,170,8,64]{1,3,2,0:T(8,128)(2,1)}, bf16[6,170,8,64]{1,3,2,0:T(8,128)(2,1)}, u32[]{:S(2)}, u32[]{:S(2)}) collective-permute-start(bf16[6,170,8,64]{1,3,2,0:T(8,128)(2,1)} %add_convert_fusion.2), channel_id=1, source_target_pairs={{0,6},{2,0},{4,2},{6,4},{1,7},{3,1},{5,3},{7,5},{8,14},{10,8},{12,... | collective-permute-start | bytes 3133448 | tf_op jit(solution)/shard_map/ppermute | solution.py:44
  104.8 168.8 %collective-permute-start.1 = (bf16[6,170,8,64]{1,3,2,0:T(8,128)(2,1)}, bf16[6,170,8,64]{1,3,2,0:T(8,128)(2,1)}, u32[]{:S(2)}, u32[]{:S(2)}) collective-permute-start(bf16[6,170,8,64]{1,3,2,0:T(8,128)(2,1)} %add_convert_fusion.2), channel_id=1, source_target_pairs={{0,4},{2,6},{4,0},{6,2},{1,5},{3,7},{5,1},{7,3},{8,12},{10,14},{12... | collective-permute-start | bytes 3133448 | tf_op jit(solution)/shard_map/ppermute | solution.py:44
  107.6 14.9 %copy-start.1 = (f32[6,170,1,512]{1,3,0,2:T(8,128)}, f32[6,170,1,512]{1,3,0,2:T(8,128)S(1)}, u32[]{:S(2)}) copy-start(f32[6,170,1,512]{1,3,0,2:T(8,128)S(1)} %copy.128) | copy-start | bytes 6266884
  109.0 13.5 %copy-start.23 = (f32[6,170,8]{1,2,0:T(8,128)}, f32[6,170,8]{1,2,0:T(8,128)S(1)}, u32[]{:S(2)}) copy-start(f32[6,170,8]{1,2,0:T(8,128)S(1)} %add_rsqrt_fusion) | copy-start | bytes 97924
  110.6 63.1 %collective-permute-start.5 = (bf16[6,170,8,64]{1,3,2,0:T(8,128)(2,1)}, bf16[6,170,8,64]{1,3,2,0:T(8,128)(2,1)}, u32[]{:S(2)}, u32[]{:S(2)}) collective-permute-start(bf16[6,170,8,64]{1,3,2,0:T(8,128)(2,1)} %multiply_convert_fusion.3), channel_id=1, source_target_pairs={{0,6},{2,0},{4,2},{6,4},{1,7},{3,1},{5,3},{7,5},{8,14},{10,8},{12,... | collective-permute-start | bytes 3133448 | tf_op jit(solution)/shard_map/ppermute | solution.py:44
  111.1 130.6 %collective-permute-start.4 = (bf16[6,170,8,64]{1,3,2,0:T(8,128)(2,1)}, bf16[6,170,8,64]{1,3,2,0:T(8,128)(2,1)}, u32[]{:S(2)}, u32[]{:S(2)}) collective-permute-start(bf16[6,170,8,64]{1,3,2,0:T(8,128)(2,1)} %multiply_convert_fusion.3), channel_id=1, source_target_pairs={{0,4},{2,6},{4,0},{6,2},{1,5},{3,7},{5,1},{7,3},{8,12},{10,14},{12... | collective-permute-start | bytes 3133448 | tf_op jit(solution)/shard_map/ppermute | solution.py:44
  112.6 129.0 %collective-permute-start.3 = (bf16[6,170,8,64]{1,3,2,0:T(8,128)(2,1)}, bf16[6,170,8,64]{1,3,2,0:T(8,128)(2,1)}, u32[]{:S(2)}, u32[]{:S(2)}) collective-permute-start(bf16[6,170,8,64]{1,3,2,0:T(8,128)(2,1)} %multiply_convert_fusion.3), channel_id=1, source_target_pairs={{0,2},{2,4},{4,6},{6,0},{1,3},{3,5},{5,7},{7,1},{8,10},{10,12},{12... | collective-permute-start | bytes 3133448 | tf_op jit(solution)/shard_map/ppermute | solution.py:44
  121.0 120.6 %copy-start.29 = (f32[6,170,8]{1,2,0:T(8,128)}, f32[6,170,8]{1,2,0:T(8,128)S(1)}, u32[]{:S(2)}) copy-start(f32[6,170,8]{1,2,0:T(8,128)S(1)} %add_rsqrt_fusion.1) | copy-start | bytes 97924
  173.7 100.0 %collective-permute-start = (bf16[6,170,8,64]{1,3,2,0:T(8,128)(2,1)}, bf16[6,170,8,64]{1,3,2,0:T(8,128)(2,1)}, u32[]{:S(2)}, u32[]{:S(2)}) collective-permute-start(bf16[6,170,8,64]{1,3,2,0:T(8,128)(2,1)} %add_convert_fusion.2), channel_id=1, source_target_pairs={{0,2},{2,4},{4,6},{6,0},{1,3},{3,5},{5,7},{7,1},{8,10},{10,12},{12... | collective-permute-start | bytes 3133448 | tf_op jit(solution)/shard_map/ppermute | solution.py:44
  241.6 17.0 %copy-start.11 = (pred[6,170,4,170]{1,3,2,0:T(8,128)(4,1)S(1)}, pred[6,170,4,170]{1,3,2,0:T(8,128)(4,1)}, u32[]{:S(2)}) copy-start(pred[6,170,4,170]{1,3,2,0:T(8,128)(4,1)} %broadcast_compare_fusion) | copy-start | bytes 2080804
  258.6 15.0 %copy-start.17 = (bf16[1,6,170,8,64]{2,4,0,3,1:T(8,128)(2,1)S(1)}, bf16[1,6,170,8,64]{2,4,0,3,1:T(8,128)(2,1)}, u32[]{:S(2)}) copy-start(bf16[1,6,170,8,64]{2,4,0,3,1:T(8,128)(2,1)} %add_convert_fusion.3) | copy-start | bytes 3133444
  311.4 12.3 %collective-permute-start.6 = (f32[1020,1024]{1,0:T(8,128)}, f32[1020,1024]{1,0:T(8,128)}, u32[]{:S(2)}, u32[]{:S(2)}) collective-permute-start(f32[1020,1024]{1,0:T(8,128)} %fusion.85), channel_id=1, source_target_pairs={{0,1},{1,0},{2,3},{3,2},{4,5},{5,4},{6,7},{7,6},{8,9},{9,8},{10,11... | collective-permute-start | bytes 12533768 | tf_op jit(solution)/shard_map/ppermute | solution.py:36
  311.4 434.6 %reduce-scatter.9.cloned.1.call-start = ((), (), s32[]{:S(2)}) async-start(), calls=%async_computation.10 | async-start | bytes 1310720 | tf_op jit(solution)/shard_map/reduce_scatter | solution.py:240
  346.3 46.4 %copy-start.18 = (bf16[1020,1024]{1,0:T(8,128)(2,1)S(1)}, bf16[1020,1024]{1,0:T(8,128)(2,1)}, u32[]{:S(2)}) copy-start(bf16[1020,1024]{1,0:T(8,128)(2,1)} %reshape.315) | copy-start | bytes 6266884
  346.3 46.4 %copy-start.57 = (f32[2048]{0:T(1024)S(1)}, f32[2048]{0:T(1024)}, u32[]{:S(2)}) copy-start(f32[2048]{0:T(1024)} %param.28) | copy-start | bytes 24580
  392.7 14.2 %copy-start.55 = (bf16[1024,2048]{1,0:T(8,128)(2,1)S(1)}, bf16[1024,2048]{1,0:T(8,128)(2,1)}, u32[]{:S(2)}) copy-start(bf16[1024,2048]{1,0:T(8,128)(2,1)} %all-gather.19.cloned.1.call-done) | copy-start | bytes 12582916
  413.1 15.2 %collective-permute-start.8 = (f32[1020,1024]{1,0:T(8,128)}, f32[1020,1024]{1,0:T(8,128)}, u32[]{:S(2)}, u32[]{:S(2)}) collective-permute-start(f32[1020,1024]{1,0:T(8,128)} %fusion.45), channel_id=1, source_target_pairs={{0,1},{1,0},{2,3},{3,2},{4,5},{5,4},{6,7},{7,6},{8,9},{9,8},{10,11... | collective-permute-start | bytes 12533768 | tf_op jit(solution)/shard_map/ppermute | solution.py:36
  421.6 17.7 %collective-permute-start.7 = (f32[1020,1024]{1,0:T(8,128)}, f32[1020,1024]{1,0:T(8,128)}, u32[]{:S(2)}, u32[]{:S(2)}) collective-permute-start(f32[1020,1024]{1,0:T(8,128)} %fusion.74), channel_id=1, source_target_pairs={{0,1},{1,0},{2,3},{3,2},{4,5},{5,4},{6,7},{7,6},{8,9},{9,8},{10,11... | collective-permute-start | bytes 12533768 | tf_op jit(solution)/shard_map/ppermute | solution.py:36
  448.6 13.2 %slice-start = ((s8[4325376]{0:T(1024)(128)(4,1)}), s8[131072]{0:T(1024)(128)(4,1)S(1)}, s32[]{:S(2)}) async-start(s8[4325376]{0:T(1024)(128)(4,1)} %bitcast.182), calls=%async_computation.17 | async-start | bytes 262144
  480.2 266.6 %reduce-scatter.11.cloned.1.call-start = ((), (), s32[]{:S(2)}) async-start(), calls=%async_computation.11 | async-start | bytes 5242880 | tf_op jit(solution)/shard_map/reduce_scatter | solution.py:239
  488.6 258.8 %reduce-scatter.13.cloned.1.call-start = ((), (), s32[]{:S(2)}) async-start(), calls=%async_computation.12 | async-start | bytes 5242880 | tf_op jit(solution)/shard_map/reduce_scatter | solution.py:241
  504.6 299.1 %reduce-scatter.7.cloned.1.call-start = ((), (), s32[]{:S(2)}) async-start(), calls=%async_computation.9 | async-start | bytes 3932160 | tf_op jit(solution)/shard_map/reduce_scatter | solution.py:238
  567.1 52.1 %collective-permute-start.12 = (bf16[6,170,8,64]{1,3,2,0:T(8,128)(2,1)}, bf16[6,170,8,64]{1,3,2,0:T(8,128)(2,1)}, u32[]{:S(2)}, u32[]{:S(2)}) collective-permute-start(bf16[6,170,8,64]{1,3,2,0:T(8,128)(2,1)} %get-tuple-element.115), channel_id=1, source_target_pairs={{0,6},{2,0},{4,2},{6,4},{1,7},{3,1},{5,3},{7,5},{8,14},{10,8},{12,... | collective-permute-start | bytes 3133448 | tf_op jit(solution)/shard_map/ppermute | solution.py:53
  569.5 69.9 %collective-permute-start.14 = (bf16[6,170,8,64]{1,3,2,0:T(8,128)(2,1)}, bf16[6,170,8,64]{1,3,2,0:T(8,128)(2,1)}, u32[]{:S(2)}, u32[]{:S(2)}) collective-permute-start(bf16[6,170,8,64]{1,3,2,0:T(8,128)(2,1)} %get-tuple-element.116), channel_id=1, source_target_pairs={{0,2},{2,4},{4,6},{6,0},{1,3},{3,5},{5,7},{7,1},{8,10},{10,12},{12... | collective-permute-start | bytes 3133448 | tf_op jit(solution)/shard_map/ppermute | solution.py:53
  569.5 71.3 %collective-permute-start.13 = (bf16[6,170,8,64]{1,3,2,0:T(8,128)(2,1)}, bf16[6,170,8,64]{1,3,2,0:T(8,128)(2,1)}, u32[]{:S(2)}, u32[]{:S(2)}) collective-permute-start(bf16[6,170,8,64]{1,3,2,0:T(8,128)(2,1)} %get-tuple-element.117), channel_id=1, source_target_pairs={{0,4},{2,6},{4,0},{6,2},{1,5},{3,7},{5,1},{7,3},{8,12},{10,14},{12... | collective-permute-start | bytes 3133448 | tf_op jit(solution)/shard_map/ppermute | solution.py:53
  570.7 30.0 %copy-start.7 = (f32[6,170,1,512]{1,3,0,2:T(8,128)S(1)}, f32[6,170,1,512]{1,3,0,2:T(8,128)}, u32[]{:S(2)}) copy-start(f32[6,170,1,512]{1,3,0,2:T(8,128)} %copy.127) | copy-start | bytes 6266884
  570.7 30.0 %copy-start.30 = (f32[6,170,8]{1,2,0:T(8,128)S(1)}, f32[6,170,8]{1,2,0:T(8,128)}, u32[]{:S(2)}) copy-start(f32[6,170,8]{1,2,0:T(8,128)} %copy-done.29) | copy-start | bytes 97924
  570.7 30.0 %copy-start.43 = (f32[8,64]{1,0:T(8,128)S(1)}, f32[8,64]{1,0:T(8,128)}, u32[]{:S(2)}) copy-start(f32[8,64]{1,0:T(8,128)} %copy-done.42) | copy-start | bytes 6148
  570.7 30.0 %copy-start.51 = (f32[8]{0:T(128)S(1)}, f32[8]{0:T(128)}, u32[]{:S(2)}) copy-start(f32[8]{0:T(128)} %copy-done.50) | copy-start | bytes 100
  616.7 55.4 %collective-permute-start.9 = (bf16[6,170,8,64]{1,3,2,0:T(8,128)(2,1)}, bf16[6,170,8,64]{1,3,2,0:T(8,128)(2,1)}, u32[]{:S(2)}, u32[]{:S(2)}) collective-permute-start(bf16[6,170,8,64]{1,3,2,0:T(8,128)(2,1)} %get-tuple-element.112), channel_id=1, source_target_pairs={{0,6},{2,0},{4,2},{6,4},{1,7},{3,1},{5,3},{7,5},{8,14},{10,8},{12,... | collective-permute-start | bytes 3133448 | tf_op jit(solution)/shard_map/ppermute | solution.py:53
  618.9 87.6 %collective-permute-start.11 = (bf16[6,170,8,64]{1,3,2,0:T(8,128)(2,1)}, bf16[6,170,8,64]{1,3,2,0:T(8,128)(2,1)}, u32[]{:S(2)}, u32[]{:S(2)}) collective-permute-start(bf16[6,170,8,64]{1,3,2,0:T(8,128)(2,1)} %get-tuple-element.113), channel_id=1, source_target_pairs={{0,2},{2,4},{4,6},{6,0},{1,3},{3,5},{5,7},{7,1},{8,10},{10,12},{12... | collective-permute-start | bytes 3133448 | tf_op jit(solution)/shard_map/ppermute | solution.py:53
  619.2 11.2 %copy-start.28 = (f32[6,170,8]{1,2,0:T(8,128)S(1)}, f32[6,170,8]{1,2,0:T(8,128)}, u32[]{:S(2)}) copy-start(f32[6,170,8]{1,2,0:T(8,128)} %copy-done.27) | copy-start | bytes 97924
  619.2 88.3 %collective-permute-start.10 = (bf16[6,170,8,64]{1,3,2,0:T(8,128)(2,1)}, bf16[6,170,8,64]{1,3,2,0:T(8,128)(2,1)}, u32[]{:S(2)}, u32[]{:S(2)}) collective-permute-start(bf16[6,170,8,64]{1,3,2,0:T(8,128)(2,1)} %get-tuple-element.114), channel_id=1, source_target_pairs={{0,4},{2,6},{4,0},{6,2},{1,5},{3,7},{5,1},{7,3},{8,12},{10,14},{12... | collective-permute-start | bytes 3133448 | tf_op jit(solution)/shard_map/ppermute | solution.py:53
  645.8 61.7 %copy-start.2 = (f32[6,170,1,512]{1,3,0,2:T(8,128)S(1)}, f32[6,170,1,512]{1,3,0,2:T(8,128)}, u32[]{:S(2)}) copy-start(f32[6,170,1,512]{1,3,0,2:T(8,128)} %copy-done.1) | copy-start | bytes 6266884
  658.5 53.4 %copy-start.26 = (f32[6,170,8]{1,2,0:T(8,128)S(1)}, f32[6,170,8]{1,2,0:T(8,128)}, u32[]{:S(2)}) copy-start(f32[6,170,8]{1,2,0:T(8,128)} %copy-done.25) | copy-start | bytes 97924
  658.5 53.5 %copy-start.24 = (f32[6,170,8]{1,2,0:T(8,128)S(1)}, f32[6,170,8]{1,2,0:T(8,128)}, u32[]{:S(2)}) copy-start(f32[6,170,8]{1,2,0:T(8,128)} %copy-done.23) | copy-start | bytes 97924
  745.9 140.0 %all-gather.25.cloned.1.call-start = ((), (), s32[]{:S(2)}) async-start(), calls=%async_computation.14 | async-start | bytes 1310720 | tf_op jit(solution)/shard_map/all_gather | solution.py:6
  746.7 219.5 %all-gather.27.cloned.1.call-start = ((), (), s32[]{:S(2)}) async-start(), calls=%async_computation.15 | async-start | bytes 5242880 | tf_op jit(solution)/shard_map/all_gather | solution.py:6
  747.3 222.0 %all-gather.29.cloned.1.call-start = ((), (), s32[]{:S(2)}) async-start(), calls=%async_computation.16 | async-start | bytes 5242880 | tf_op jit(solution)/shard_map/all_gather | solution.py:6
  748.0 240.8 %all-gather.23.cloned.1.call-start = ((), (), s32[]{:S(2)}) async-start(), calls=%async_computation.13 | async-start | bytes 3932160 | tf_op jit(solution)/shard_map/all_gather | solution.py:6
  748.0 55.8 %copy-start.37 = (f32[6,1024]{1,0:T(8,128)S(1)}, f32[6,1024]{1,0:T(8,128)}, u32[]{:S(2)}) copy-start(f32[6,1024]{1,0:T(8,128)} %get-tuple-element.87) | copy-start | bytes 73732
  748.1 55.8 %copy-start.36 = (f32[6,1024]{1,0:T(8,128)S(1)}, f32[6,1024]{1,0:T(8,128)}, u32[]{:S(2)}) copy-start(f32[6,1024]{1,0:T(8,128)} %get-tuple-element.91) | copy-start | bytes 73732
  748.1 55.8 %copy-start.38 = (f32[6,1024]{1,0:T(8,128)S(1)}, f32[6,1024]{1,0:T(8,128)}, u32[]{:S(2)}) copy-start(f32[6,1024]{1,0:T(8,128)} %get-tuple-element.80) | copy-start | bytes 73732
  748.1 55.9 %copy-start.59 = (f32[8]{0:T(128)S(1)}, f32[8]{0:T(128)}, u32[]{:S(2)}) copy-start(f32[8]{0:T(128)} %param.24) | copy-start | bytes 100
  748.1 56.0 %copy-start.46 = (f32[1024]{0:T(1024)S(1)}, f32[1024]{0:T(1024)}, u32[]{:S(2)}) copy-start(f32[1024]{0:T(1024)} %get-tuple-element.94) | copy-start | bytes 12292
  748.1 56.0 %copy-start.48 = (f32[2048]{0:T(1024)S(1)}, f32[2048]{0:T(1024)}, u32[]{:S(2)}) copy-start(f32[2048]{0:T(1024)} %get-tuple-element.95) | copy-start | bytes 24580
  755.5 132.7 %collective-permute-start.15 = (f32[1020,1024]{1,0:T(8,128)}, f32[1020,1024]{1,0:T(8,128)}, u32[]{:S(2)}, u32[]{:S(2)}) collective-permute-start(f32[1020,1024]{1,0:T(8,128)} %fusion.87), channel_id=1, source_target_pairs={{0,1},{1,0},{2,3},{3,2},{4,5},{5,4},{6,7},{7,6},{8,9},{9,8},{10,11... | collective-permute-start | bytes 12533768 | tf_op jit(solution)/shard_map/ppermute | solution.py:36
  944.7 20.8 %all-to-all-start = ((f32[4,6,256]{2,1,0:T(8,128)}), f32[4,6,256]{2,1,0:T(8,128)S(1)}, u32[]{:S(2)}, u32[]{:S(2)}) async-start(f32[4,6,256]{2,1,0:T(8,128)} %fusion.88), calls=%async_computation | async-start | bytes 65536 | tf_op jit(solution)/shard_map/all_to_all | solution.py:234
  (30 other events, 127.6 us)
Sparse Core Ops, SparseCore 0:
  10.1 79.1 all-gather.14
  90.9 31.7 all-gather.16
  124.3 79.0 all-gather.18
  311.5 81.0 all-gather.20
  480.3 25.6 reduce-scatter.8
  508.1 75.2 reduce-scatter.10
  585.7 77.2 reduce-scatter.12
  746.1 57.6 reduce-scatter.6
  805.6 26.7 all-gather.24
  834.1 53.0 all-gather.26
  889.1 54.3 all-gather.28
  945.2 43.5 all-gather.22
